TPU v7x, 1024 devices: a whole 4x8x16 slice. The times are simulated.
1024 devices in a mesh: section: 16 (over y, z_hi), dp: 8 (over x, core), tensor: 8 (over z_lo).
Axes of the slice: x: 4, y: 8, z: 16 (z_hi: 2, z_lo: 8; z = z_hi * 8 + z_lo), core: 2. Of those that a mesh axis runs over, the one named last changes fastest.
Arguments:
- queries: bfloat16 [16, 8192, 4096], P('section', ('dp', 'tensor')), parts along dimension 1, may hold values from -50 to 50
- keys_values: bfloat16 [16, 8192, 4, 256], P('section', ('dp', 'tensor')), parts along dimension 1, may hold values from -5 to 5
- segment_ids: int32 [16, 8192], P('section', ('dp', 'tensor')), parts along dimension 1, may hold values from 0 to 3, never falling along the last dimension, each value on 1 to 640 neighbouring positions
- bounds: int32 [16, 32], P('section', 'dp'), parts along dimension 1, may hold values from 0 to 1023
Outputs:
- received: bfloat16 [16, 8192, 4096], P('section', ('dp', 'tensor')), parts along dimension 1
There are 8 independent parts, one for each index of `dp`. A program takes and returns all parts, laid end to end along the dimension named above; each array names one. Nothing has to cross between parts.
Inputs may be any that keep to these rules, and one draw needn't show every extreme that they name: `segment_ids`: segment numbers never fall along a micro-batch; each document has 1 to 640 tokens and one has exactly 640.
All inputs are finite; a program needn't handle non-finite values.
Results may differ from a plain program's by a relative error of at most 0.0037.
Values may be sent and summed in bfloat16 or wider, within the bound.
No kernel may reach another device: no remote copies, remote signals or barrier semaphores. Data moves between devices by JAX's collectives and lax.ppermute only.
A program may use at most 64 MiB of HBM per device.

v0:
```python
import math

import jax
import jax.numpy as jnp
from jax import lax
from jax.sharding import PartitionSpec as P


def from_behind(block, axis, distance):
    devices = range(lax.axis_size(axis))
    route = [((i - distance) % len(devices), i) for i in devices]
    return lax.ppermute(block, axis, route)


def bound_of(segments, limits):
    levels = jnp.arange(limits.shape[0])
    return jnp.sum(jnp.where(segments[:, None] == levels[None, :], limits[None, :], 0), axis=1)


def shards(queries, keys_values, segment_ids, bounds):
    query_rows = queries[0]
    pairs = keys_values[0]
    segments = segment_ids[0]
    limits = bounds[0]
    rows = query_rows.shape[0]
    kv_heads = pairs.shape[1]
    head_size = pairs.shape[2] // 2
    heads = query_rows.shape[1] // head_size
    groups = heads // kv_heads
    scale = 1.0 / math.sqrt(head_size)
    segment_wire = segments.astype(jnp.bfloat16)
    my_first = lax.axis_index("tensor") * rows
    query_pos = my_first + jnp.arange(rows)
    query_bound = bound_of(segments, limits)
    shaped = query_rows.reshape(rows, kv_heads, groups, head_size)
    start_max = jnp.full((kv_heads, groups, rows), -1e30, jnp.float32)
    running = start_max
    pair_piece = lax.all_gather(pairs, "tensor", axis=0, tiled=True)
    segment_piece = lax.all_gather(segment_wire, "tensor", axis=0, tiled=True)
    count = pair_piece.shape[0]
    key_pos = jnp.arange(count)
    key_segment = segment_piece.astype(jnp.int32)
    visible = (segments[:, None] == key_segment[None, :]) & (
        (key_pos[None, :] <= query_pos[:, None]) | (key_pos[None, :] <= query_bound[:, None])
    )
    mask_bias = jnp.where(visible, 0.0, -1e30).astype(jnp.float32)
    scores = (
        jnp.einsum(
            "rhgd,nhd->hgrn",
            shaped,
            pair_piece[:, :, :head_size],
            preferred_element_type=jnp.float32,
        )
        * scale
        + mask_bias[None, None]
    )
    updated = jnp.maximum(running, jnp.max(scores, axis=-1))
    weight = jnp.exp(scores - updated[..., None])
    total = jnp.sum(weight, axis=-1)
    summed = jnp.einsum(
        "hgrn,nhd->hgrd",
        weight.astype(jnp.bfloat16),
        pair_piece[:, :, head_size:],
        preferred_element_type=jnp.float32,
    )
    running, total, summed = (updated, total, summed)
    result = (
        jnp.transpose(summed / total[..., None], (2, 0, 1, 3))
        .reshape(rows, heads * head_size)
        .astype(jnp.bfloat16)
    )
    return from_behind(result[None], "section", 1)


def solution(mesh):
    in_specs = (
        P("section", ("dp", "tensor"), None),
        P("section", ("dp", "tensor"), None, None),
        P("section", ("dp", "tensor")),
        P("section", "dp"),
    )
    out_specs = P("section", ("dp", "tensor"), None)
    return jax.shard_map(shards, mesh=mesh, in_specs=in_specs, out_specs=out_specs, check_vma=False)
```

profile of v0, /device:TPU:1, one launch (start us, length us, event | category | flops | bytes accessed | tf_op | source)
XLA Modules:
  0.0 224.2 jit_solution(15706368076254662046)
XLA Ops:
  6.5 0.0 all-gather.4.cloned.1.call-start
  6.5 1.7 copy.15
  8.2 0.0 all-gather.4.cloned.1.call-update
  8.2 0.7 convert_bitcast_fusion
  8.9 35.6 %all-gather.1 = bf16[8,1,128]{2,1,0:T(2,128)(2,1)S(1)} all-gather(bf16[1,1,128]{2,1,0:T(2,128)(2,1)S(1)} %convert_bitcast_fusion), channel_id=1, replica_groups=mesh['section'=16,'dp'=8,'tensor'=8] {'tensor'}, dimensions={0}, use_global_device_ids=true | all-gather | bytes 2304 | tf_op jit(solution)/shard_map/all_gather | solution.py:39
  44.5 1.4 copy.25
  46.0 0.8 select_reduce_fusion
  46.7 0.9 fusion.12
  47.6 40.0 %all-gather.4.cloned.1.call-done = bf16[1,1024,4,256]{3,1,2,0:T(8,128)(2,1)} async-done(((bf16[1,128,4,256]{3,1,2,0:T(8,128)(2,1)}), bf16[1,1024,4,256]{3,1,2,0:T(8,128)(2,1)}) %all-gather.4.cloned.1.call-update) | async-done | bytes 2097168 | tf_op jit(solution)/shard_map/all_gather | solution.py:38
  87.6 8.3 %fusion.2 = (f32[4,8,128]{2,1,0:T(8,128)S(1)}, f32[4,1024,128,8]{2,1,3,0:T(8,128)}) fusion(f32[128,1024]{0,1:T(8,128)S(1)} %fusion.12, bf16[128,4,8,128]{3,2,1,0:T(8,128)(2,1)S(1)} %bitcast.40, bf16[1024,4,256]{2,0,1:T(8,128)(2,1)} %bitcast.43), kind=kOutput, calls=%fused_computation.4 | convolution fusion | flops 1086320640 | bytes 19415040 | tf_op jit(solution)/shard_map/rhgd,nhd->hgrn/dot_general | solution.py:48
  95.9 9.2 %fusion = f32[4,8,128]{2,1,0:T(8,128)S(1)} fusion(f32[4,1024,128,8]{2,1,3,0:T(8,128)} %get-tuple-element.6, f32[4,8,128]{2,1,0:T(8,128)S(1)} %broadcast_maximum_fusion, f32[128,1024]{0,1:T(8,128)S(1)} %fusion.12), kind=kLoop, calls=%fused_computation.2 | loop fusion | flops 16773120 | bytes 17334272 | tf_op jit(solution)/shard_map/reduce_sum | solution.py:59
  105.1 9.7 %fusion.5 = bf16[128,4,8,128]{0,3,2,1:T(8,128)(2,1)S(1)} fusion(f32[4,1024,128,8]{2,1,3,0:T(8,128)} %get-tuple-element.6, f32[4,8,128]{2,1,0:T(8,128)S(1)} %broadcast_maximum_fusion, f32[128,1024]{0,1:T(8,128)S(1)} %fusion.12, bf16[1024,4,256]{2,0,1:T(8,128)(2,1)} %bitcast.44, f32[128,4,8]{0,2,1:T(8,128)S(1)} %bitcast.46), kind=kOutput, calls=%fused_computation.7 | convolution fusion | flops 1091567616 | bytes 19431424 | tf_op jit(solution)/shard_map/hgrn,nhd->hgrd/dot_general | solution.py:60
  114.8 0.5 copy.19
  115.4 8.5 %collective-permute-start = (bf16[1,128,4096]{2,1,0:T(8,128)(2,1)S(1)}, bf16[1,128,4096]{2,1,0:T(8,128)(2,1)S(1)}, u32[]{:S(2)}, u32[]{:S(2)}) collective-permute-start(bf16[1,128,4096]{2,1,0:T(8,128)(2,1)S(1)} %copy.19), channel_id=1, source_target_pairs={{960,0},{0,64},{64,128},{128,192},{192,256},{256,320},{320,384},{3... | collective-permute-start | bytes 3145736 | tf_op jit(solution)/shard_map/ppermute | solution.py:12
  123.9 92.5 %collective-permute-done = bf16[1,128,4096]{2,1,0:T(8,128)(2,1)S(1)} collective-permute-done((bf16[1,128,4096]{2,1,0:T(8,128)(2,1)S(1)}, bf16[1,128,4096]{2,1,0:T(8,128)(2,1)S(1)}, u32[]{:S(2)}, u32[]{:S(2)}) %collective-permute-start) | collective-permute-done | bytes 1048608 | tf_op jit(solution)/shard_map/ppermute | solution.py:12
  216.4 1.0 copy.31
  (3 shorter events, 0.0 us)
Async XLA Ops:
  6.5 81.0 %all-gather.4.cloned.1.call-start = ((), (), s32[]{:S(2)}) async-start(), calls=%async_computation | async-start | bytes 2359296 | tf_op jit(solution)/shard_map/all_gather | solution.py:38
  115.4 101.1 %collective-permute-start = (bf16[1,128,4096]{2,1,0:T(8,128)(2,1)S(1)}, bf16[1,128,4096]{2,1,0:T(8,128)(2,1)S(1)}, u32[]{:S(2)}, u32[]{:S(2)}) collective-permute-start(bf16[1,128,4096]{2,1,0:T(8,128)(2,1)S(1)} %copy.19), channel_id=1, source_target_pairs={{960,0},{0,64},{64,128},{128,192},{192,256},{256,320},{320,384},{3... | collective-permute-start | bytes 3145736 | tf_op jit(solution)/shard_map/ppermute | solution.py:12
Sparse Core Ops, SparseCore 0:
  10.0 77.5 all-gather.3
where the time goes:
time: 225 us; the launch traced here: 224 us
  waiting for transfers between devices  133 us (59%)
  blocking collectives  35.6 us (16%)
  matrix products  18.1 us (8%)
  between operations  13.5 us (6%)
  other arithmetic  11.5 us (5%)
  starting transfers between devices  8.54 us (4%)
  local copies, waits for them, and re-layouts  4.62 us (2%)
    ppermute x1, waiting for transfers between devices, from_behind(): return lax.ppermute(block, axis, route)  92.5 us
    all_gather x1, waiting for transfers between devices, shards(): pair_piece = lax.all_gather(pairs, 'tensor', axis=0, tiled=True)  40 us
    all_gather x1, blocking collectives, shards(): segment_piece = lax.all_gather(segment_wire, 'tensor', axis=0, tiled=True)  35.6 us
    dot_general x1, matrix products, shards(): jnp.einsum('hgrn,nhd->hgrd', weight.astype(jnp.bfloat16), pair_piece[:, :...  9.72 us
    reduce_sum x1, other arithmetic, shards(): total = jnp.sum(weight, axis=-1)  9.17 us
    ppermute x1, starting transfers between devices, from_behind(): return lax.ppermute(block, axis, route)  8.54 us
    dot_general x1, matrix products, shards(): jnp.einsum('rhgd,nhd->hgrn', shaped, pair_piece[:, :, :head_size], prefer...  8.33 us
  transfers between devices with their start and end apart: 2, of which 2 were waited for; matrix products, arithmetic and copies ran while one was open for 2% of the time, Pallas kernels for 0%

commit v1 on v0

v1 whole, which is shorter than its diff:
```python
import math

import jax
import jax.numpy as jnp
from jax import lax
from jax.sharding import PartitionSpec as P


def from_behind(block, axis, distance):
    devices = range(lax.axis_size(axis))
    route = [((i - distance) % len(devices), i) for i in devices]
    return lax.ppermute(block, axis, route)


def bound_of(segments, limits):
    levels = jnp.arange(limits.shape[0])
    return jnp.sum(jnp.where(segments[:, None] == levels[None, :], limits[None, :], 0), axis=1)


def attend(queries, keys_values, segment_ids, bounds):
    query_rows = queries[0]
    pairs = keys_values[0]
    segments = segment_ids[0]
    limits = bounds[0]
    rows = query_rows.shape[0]
    kv_heads = pairs.shape[1]
    width = pairs.shape[2]
    head_size = width // 2
    heads = query_rows.shape[1] // head_size
    groups = heads // kv_heads
    scale = 1.0 / math.sqrt(head_size)
    lane = 128
    tensor_size = lax.axis_size("tensor")
    my_first = lax.axis_index("tensor") * rows
    query_pos = my_first + jnp.arange(rows)
    query_bound = bound_of(segments, limits)
    shaped = query_rows.reshape(rows, kv_heads, groups, head_size)

    flat = pairs.reshape(rows * kv_heads * width // lane, lane)
    pad_rows = 16
    seg_block = jnp.zeros((pad_rows, lane), jnp.bfloat16)
    seg_block = seg_block.at[: rows // lane].set(segments.astype(jnp.bfloat16).reshape(rows // lane, lane))
    packed = jnp.concatenate([flat, seg_block], axis=0)
    gathered = lax.all_gather(packed, "tensor", axis=0, tiled=False)
    body_rows = flat.shape[0]
    pair_piece = gathered[:, :body_rows].reshape(tensor_size * rows, kv_heads, width)
    key_segment = gathered[:, body_rows : body_rows + rows // lane].reshape(tensor_size * rows).astype(jnp.int32)

    count = pair_piece.shape[0]
    key_pos = jnp.arange(count)
    visible = (segments[:, None] == key_segment[None, :]) & (
        (key_pos[None, :] <= query_pos[:, None]) | (key_pos[None, :] <= query_bound[:, None])
    )
    mask_bias = jnp.where(visible, 0.0, -1e30).astype(jnp.float32)

    pieces = []
    for h in range(kv_heads):
      q_h = shaped[:, h]
      k_h = pair_piece[:, h, :head_size]
      v_h = pair_piece[:, h, head_size:]
      scores = (
          jnp.einsum("rgd,nd->grn", q_h, k_h, preferred_element_type=jnp.float32) * scale
          + mask_bias[None]
      )
      largest = jnp.max(scores, axis=-1)
      weight = jnp.exp(scores - largest[..., None])
      total = jnp.sum(weight, axis=-1)
      summed = jnp.einsum(
          "grn,nd->grd", weight.astype(jnp.bfloat16), v_h, preferred_element_type=jnp.float32
      )
      out_h = (
          jnp.transpose(summed / total[..., None], (1, 0, 2))
          .reshape(rows, groups * head_size)
          .astype(jnp.bfloat16)
      )
      pieces.append(from_behind(out_h, "section", 1))
    result = jnp.concatenate(pieces, axis=1)
    return result[None]


def solution(mesh):
    in_specs = (
        P("section", ("dp", "tensor"), None),
        P("section", ("dp", "tensor"), None, None),
        P("section", ("dp", "tensor")),
        P("section", "dp"),
    )
    out_specs = P("section", ("dp", "tensor"), None)
    return jax.shard_map(attend, mesh=mesh, in_specs=in_specs, out_specs=out_specs, check_vma=False)
```

time: 225 us -> 238 us (1.058)
  blocking collectives: 35.6 us -> 0 us
  starting transfers between devices: 8.54 us -> 29.7 us
  local copies, waits for them, and re-layouts: 4.62 us -> 20 us
  waiting for transfers between devices: 133 us -> 148 us
  matrix products: 18.1 us -> 15.7 us
    all_gather x1, waiting for transfers between devices: 40 us -> 76.2 us  [attend(): gathered = lax.all_gather(packed, 'tensor', axis=0, tiled=False)]
    all_gather x1 -> x0, blocking collectives: 35.6 us -> none  [shards(): segment_piece = lax.all_gather(segment_wire, 'tensor', axis=0, tiled=True)]
    ppermute x1 -> x4, starting transfers between devices: 8.54 us -> 29.7 us  [from_behind(): return lax.ppermute(block, axis, route)]
    ppermute x1 -> x4, waiting for transfers between devices: 92.5 us -> 72.2 us  [from_behind(): return lax.ppermute(block, axis, route)]
    slice x0 -> x2, local copies, waits for them, and re-layouts: none -> 7.67 us  [the longest x1 4.63 us: attend(): v_h = pair_piece[:, h, head_size:]]
    unnamed x3 -> x21, local copies, waits for them, and re-layouts: 4.09 us -> 7.57 us
    reshape x0 -> x1, local copies, waits for them, and re-layouts: none -> 3.15 us  [attend(): gathered[:, :body_rows].reshape(tensor_size * rows, kv_heads, width)]
    reduce_sum x1, other arithmetic: 9.17 us -> 6.07 us  [attend(): total = jnp.sum(weight, axis=-1)]
  transfers between devices with their start and end apart: 2 -> 5, of which waited for: 2 -> 5; matrix products, arithmetic and copies ran while one was open for 2% -> 1% of each run, Pallas kernels for 0% -> 0%
where the time goes in v1:
time: 238 us
  waiting for transfers between devices  148 us (62%)
  starting transfers between devices  29.7 us (12%)
  local copies, waits for them, and re-layouts  20 us (8%)
  matrix products  15.7 us (7%)
  between operations  13.7 us (6%)
  other arithmetic  10.2 us (4%)
    all_gather x1, waiting for transfers between devices, attend(): gathered = lax.all_gather(packed, 'tensor', axis=0, tiled=False)  76.2 us
    ppermute x4, waiting for transfers between devices, from_behind(): return lax.ppermute(block, axis, route)  72.2 us
    ppermute x4, starting transfers between devices, from_behind(): return lax.ppermute(block, axis, route)  29.7 us
    dot_general x4, matrix products, attend(): jnp.einsum('grn,nd->grd', weight.astype(jnp.bfloat16), v_h, preferred_ele...  8.5 us
    unnamed x21, local copies, waits for them, and re-layouts  7.57 us
    dot_general x4, matrix products, attend(): jnp.einsum('rgd,nd->grn', q_h, k_h, preferred_element_type=jnp.float32)  7.19 us
    reduce_sum x1, other arithmetic, attend(): total = jnp.sum(weight, axis=-1)  6.07 us
  transfers between devices with their start and end apart: 5, of which 5 were waited for; matrix products, arithmetic and copies ran while one was open for 1% of the time, Pallas kernels for 0%

profile of v1, /device:TPU:1, one launch (start us, length us, event | category | flops | bytes accessed | tf_op | source)
XLA Modules:
  0.0 237.6 jit_solution(11309405724625291133)
XLA Ops:
  6.5 0.7 convert_element_type.50
  7.2 1.1 reshape_squeeze.6
  8.2 0.7 fusion.60
  9.0 1.6 copy.39
  10.6 0.8 select_reduce_fusion
  11.4 76.2 %all-gather.3.cloned.1.call-done = bf16[8320,128]{1,0:T(8,128)(2,1)} async-done(((bf16[1040,128]{1,0:T(8,128)(2,1)}), bf16[8320,128]{1,0:T(8,128)(2,1)}) %all-gather.3.cloned.1.call-update) | async-done | bytes 2129936 | tf_op jit(solution)/shard_map/all_gather | solution.py:44
  87.6 0.7 slice_convert_fusion
  88.3 3.0 %slice.72 = bf16[8,1024,128]{2,1,0:T(8,128)(2,1)} slice(bf16[8,1040,128]{2,1,0:T(8,128)(2,1)} %bitcast.160), slice={[0:8], [0:1024], [0:128]} | slice | bytes 4194304 | tf_op jit(solution)/shard_map/slice | solution.py:46
  91.4 3.1 %reshape.127 = bf16[1024,4,256]{2,1,0:T(4,128)(2,1)S(1)} reshape(bf16[8,1024,128]{2,1,0:T(8,128)(2,1)} %slice.72) | data formatting | bytes 4194304 | tf_op jit(solution)/shard_map/reshape | solution.py:46
  94.5 4.6 %fusion.73 = (bf16[1024,1,128]{2,1,0:T(2,128)(2,1)}, bf16[1024,1,128]{2,1,0:T(2,128)(2,1)}, bf16[1024,1,128]{2,1,0:T(2,128)(2,1)}, bf16[1024,1,128]{2,1,0:T(2,12...) fusion(bf16[1024,4,256]{2,1,0:T(4,128)(2,1)S(1)} %reshape.127), kind=kLoop, calls=%fused_computation.69 | loop fusion | bytes 4194304 | tf_op jit(solution)/shard_map/slice | solution.py:60
  99.2 1.9 copy.63
  101.1 1.2 copy.69
  102.4 1.2 copy.66
  103.6 1.2 copy.72
  104.9 1.8 fusion.62
  106.7 0.7 fusion.61
  107.6 0.7 fusion.8
  108.6 4.0 %fusion = (f32[8,128]{1,0:T(8,128)S(1)}, f32[8,128]{1,0:T(8,128)S(1)}, f32[8,128]{1,0:T(8,128)S(1)}, f32[8,128]{1,0:T(8,128)S(1)}, f32[1024,128,8]{1,0,2:T(8,128)}) fusion(f32[1024,128,8]{1,0,2:T(8,128)S(1)} %get-tuple-element.33, f32[8,128]{1,0:T(8,128)S(1)} %get-tuple-element.32, f32[128,1024]{0,1:T(8,128)S(1)} %fusion.59, ...), kind=kOutput, calls=%fused_computation.8 | convolution fusion | flops 282062848 | bytes 18108416 | tf_op jit(solution)/shard_map/rgd,nd->grn/dot_general | solution.py:62
  112.6 1.0 fusion.53
  113.8 6.1 %fusion.2 = (f32[8,128]{1,0:T(8,128)S(1)}, f32[8,128]{1,0:T(8,128)S(1)}, f32[8,128]{1,0:T(8,128)S(1)}) fusion(f32[1024,128,8]{1,0,2:T(8,128)} %get-tuple-element.34, f32[8,128]{1,0:T(8,128)S(1)} %get-tuple-element.18, f32[128,1024]{0,1:T(8,128)S(1)} %fusion.59, f32[8,128]{1,0:T(8,128)S(1)} %get-tuple-element.19, f32[1024,128,8]{1,0,2:T(8,128)} %copy-done, ...), kind=kLoop, calls=%fused_computation.10 | loop fusion | flops 12579840 | bytes 13131776 | tf_op jit(solution)/shard_map/reduce_sum | solution.py:67
  119.9 1.1 fusion.35
  121.1 3.2 %fusion.47 = bf16[128,8,128]{0,2,1:T(8,128)(2,1)S(1)} fusion(f32[1024,128,8]{1,0,2:T(8,128)} %get-tuple-element.34, f32[8,128]{1,0:T(8,128)S(1)} %get-tuple-element.18, f32[128,1024]{0,1:T(8,128)S(1)} %fusion.59, bf16[1024,1,128]{0,2,1:T(8,128)(2,1)S(1)} %copy.66, f32[128,8]{0,1:T(8,128)S(1)} %bitcast.167), kind=kOutput, calls=%fused_computation.33 | convolution fusion | flops 272891904 | bytes 5251072 | tf_op jit(solution)/shard_map/grn,nd->grd/dot_general | solution.py:68
  124.5 3.2 %fusion.41 = bf16[128,8,128]{0,2,1:T(8,128)(2,1)S(1)} fusion(f32[1024,128,8]{1,0,2:T(8,128)} %copy-done, f32[8,128]{1,0:T(8,128)S(1)} %get-tuple-element.19, f32[128,1024]{0,1:T(8,128)S(1)} %fusion.59, bf16[1024,1,128]{0,2,1:T(8,128)(2,1)S(1)} %copy.69, f32[128,8]{0,1:T(8,128)S(1)} %bitcast.166), kind=kOutput, calls=%fused_computation.31 | convolution fusion | flops 272891904 | bytes 5251072 | tf_op jit(solution)/shard_map/grn,nd->grd/dot_general | solution.py:68
  127.9 8.8 %collective-permute-start.2 = (bf16[128,1024]{1,0:T(8,128)(2,1)S(1)}, bf16[128,1024]{1,0:T(8,128)(2,1)S(1)}, u32[]{:S(2)}, u32[]{:S(2)}) collective-permute-start(bf16[128,1024]{1,0:T(8,128)(2,1)S(1)} %copy.53), channel_id=1, source_target_pairs={{960,0},{0,64},{64,128},{128,192},{192,256},{256,320},{320,384},{3... | collective-permute-start | bytes 786440 | tf_op jit(solution)/shard_map/ppermute | solution.py:12
  136.6 6.0 %collective-permute-start.1 = (bf16[128,1024]{1,0:T(8,128)(2,1)S(1)}, bf16[128,1024]{1,0:T(8,128)(2,1)S(1)}, u32[]{:S(2)}, u32[]{:S(2)}) collective-permute-start(bf16[128,1024]{1,0:T(8,128)(2,1)S(1)} %copy.48), channel_id=1, source_target_pairs={{960,0},{0,64},{64,128},{128,192},{192,256},{256,320},{320,384},{3... | collective-permute-start | bytes 786440 | tf_op jit(solution)/shard_map/ppermute | solution.py:12
  142.7 8.9 %collective-permute-start.3 = (bf16[128,1024]{1,0:T(8,128)(2,1)S(1)}, bf16[128,1024]{1,0:T(8,128)(2,1)S(1)}, u32[]{:S(2)}, u32[]{:S(2)}) collective-permute-start(bf16[128,1024]{1,0:T(8,128)(2,1)S(1)} %copy.58), channel_id=1, source_target_pairs={{960,0},{0,64},{64,128},{128,192},{192,256},{256,320},{320,384},{3... | collective-permute-start | bytes 786440 | tf_op jit(solution)/shard_map/ppermute | solution.py:12
  151.6 6.0 %collective-permute-start = (bf16[128,1024]{1,0:T(8,128)(2,1)S(1)}, bf16[128,1024]{1,0:T(8,128)(2,1)S(1)}, u32[]{:S(2)}, u32[]{:S(2)}) collective-permute-start(bf16[128,1024]{1,0:T(8,128)(2,1)S(1)} %copy.43), channel_id=1, source_target_pairs={{960,0},{0,64},{64,128},{128,192},{192,256},{256,320},{320,384},{3... | collective-permute-start | bytes 786440 | tf_op jit(solution)/shard_map/ppermute | solution.py:12
  157.6 46.6 %collective-permute-done.2 = bf16[128,1024]{1,0:T(8,128)(2,1)S(1)} collective-permute-done((bf16[128,1024]{1,0:T(8,128)(2,1)S(1)}, bf16[128,1024]{1,0:T(8,128)(2,1)S(1)}, u32[]{:S(2)}, u32[]{:S(2)}) %collective-permute-start.2) | collective-permute-done | bytes 262176 | tf_op jit(solution)/shard_map/ppermute | solution.py:12
  204.2 14.3 %collective-permute-done.1 = bf16[128,1024]{1,0:T(8,128)(2,1)S(1)} collective-permute-done((bf16[128,1024]{1,0:T(8,128)(2,1)S(1)}, bf16[128,1024]{1,0:T(8,128)(2,1)S(1)}, u32[]{:S(2)}, u32[]{:S(2)}) %collective-permute-start.1) | collective-permute-done | bytes 262176 | tf_op jit(solution)/shard_map/ppermute | solution.py:12
  218.5 5.6 %collective-permute-done.3 = bf16[128,1024]{1,0:T(8,128)(2,1)S(1)} collective-permute-done((bf16[128,1024]{1,0:T(8,128)(2,1)S(1)}, bf16[128,1024]{1,0:T(8,128)(2,1)S(1)}, u32[]{:S(2)}, u32[]{:S(2)}) %collective-permute-start.3) | collective-permute-done | bytes 262176 | tf_op jit(solution)/shard_map/ppermute | solution.py:12
  224.1 5.6 %collective-permute-done = bf16[128,1024]{1,0:T(8,128)(2,1)S(1)} collective-permute-done((bf16[128,1024]{1,0:T(8,128)(2,1)S(1)}, bf16[128,1024]{1,0:T(8,128)(2,1)S(1)}, u32[]{:S(2)}, u32[]{:S(2)}) %collective-permute-start) | collective-permute-done | bytes 262176 | tf_op jit(solution)/shard_map/ppermute | solution.py:12
  229.7 1.0 maximum_bitcast_fusion
  (24 shorter events, 1.1 us)
Async XLA Ops:
  6.5 81.1 %all-gather.3.cloned.1.call-start = ((), (), s32[]{:S(2)}) async-start(), calls=%async_computation | async-start | bytes 2396160 | tf_op jit(solution)/shard_map/all_gather | solution.py:44
  99.2 7.5 %copy-start.5 = (bf16[1024,1,128]{2,1,0:T(2,128)(2,1)S(1)}, bf16[1024,1,128]{2,1,0:T(2,128)(2,1)}, u32[]{:S(2)}) copy-start(bf16[1024,1,128]{2,1,0:T(2,128)(2,1)} %get-tuple-element.30) | copy-start | bytes 786436
  104.9 2.6 %copy-start.7 = (s32[1,128]{1,0:T(1,128)S(1)}, s32[1,128]{1,0:T(1,128)}, u32[]{:S(2)}) copy-start(s32[1,128]{1,0:T(1,128)} %param.8) | copy-start | bytes 1540
  104.9 2.8 %copy-start.4 = (bf16[1024,1,128]{2,1,0:T(2,128)(2,1)S(1)}, bf16[1024,1,128]{2,1,0:T(2,128)(2,1)}, u32[]{:S(2)}) copy-start(bf16[1024,1,128]{2,1,0:T(2,128)(2,1)} %get-tuple-element.29) | copy-start | bytes 786436
  106.7 1.9 copy-start
  106.7 1.9 copy-start.3
  107.4 5.2 %copy-start.1 = (f32[1024,128,8]{1,0,2:T(8,128)}, f32[1024,128,8]{1,0,2:T(8,128)S(1)}, u32[]{:S(2)}) copy-start(f32[1024,128,8]{1,0,2:T(8,128)S(1)} %fusion.61) | copy-start | bytes 12582916
  108.6 4.0 %copy-start.6 = (bf16[1024,1,128]{0,2,1:T(8,128)(2,1)S(1)}, bf16[1024,1,128]{0,2,1:T(8,128)(2,1)}, u32[]{:S(2)}) copy-start(bf16[1024,1,128]{0,2,1:T(8,128)(2,1)} %copy.63) | copy-start | bytes 786436
  113.8 6.1 %copy-start.2 = (f32[1024,128,8]{1,0,2:T(8,128)S(1)}, f32[1024,128,8]{1,0,2:T(8,128)}, u32[]{:S(2)}) copy-start(f32[1024,128,8]{1,0,2:T(8,128)} %copy-done.1) | copy-start | bytes 12582916
  127.9 76.3 %collective-permute-start.2 = (bf16[128,1024]{1,0:T(8,128)(2,1)S(1)}, bf16[128,1024]{1,0:T(8,128)(2,1)S(1)}, u32[]{:S(2)}, u32[]{:S(2)}) collective-permute-start(bf16[128,1024]{1,0:T(8,128)(2,1)S(1)} %copy.53), channel_id=1, source_target_pairs={{960,0},{0,64},{64,128},{128,192},{192,256},{256,320},{320,384},{3... | collective-permute-start | bytes 786440 | tf_op jit(solution)/shard_map/ppermute | solution.py:12
  136.6 81.9 %collective-permute-start.1 = (bf16[128,1024]{1,0:T(8,128)(2,1)S(1)}, bf16[128,1024]{1,0:T(8,128)(2,1)S(1)}, u32[]{:S(2)}, u32[]{:S(2)}) collective-permute-start(bf16[128,1024]{1,0:T(8,128)(2,1)S(1)} %copy.48), channel_id=1, source_target_pairs={{960,0},{0,64},{64,128},{128,192},{192,256},{256,320},{320,384},{3... | collective-permute-start | bytes 786440 | tf_op jit(solution)/shard_map/ppermute | solution.py:12
  142.7 81.5 %collective-permute-start.3 = (bf16[128,1024]{1,0:T(8,128)(2,1)S(1)}, bf16[128,1024]{1,0:T(8,128)(2,1)S(1)}, u32[]{:S(2)}, u32[]{:S(2)}) collective-permute-start(bf16[128,1024]{1,0:T(8,128)(2,1)S(1)} %copy.58), channel_id=1, source_target_pairs={{960,0},{0,64},{64,128},{128,192},{192,256},{256,320},{320,384},{3... | collective-permute-start | bytes 786440 | tf_op jit(solution)/shard_map/ppermute | solution.py:12
  151.6 78.2 %collective-permute-start = (bf16[128,1024]{1,0:T(8,128)(2,1)S(1)}, bf16[128,1024]{1,0:T(8,128)(2,1)S(1)}, u32[]{:S(2)}, u32[]{:S(2)}) collective-permute-start(bf16[128,1024]{1,0:T(8,128)(2,1)S(1)} %copy.43), channel_id=1, source_target_pairs={{960,0},{0,64},{64,128},{128,192},{192,256},{256,320},{320,384},{3... | collective-permute-start | bytes 786440 | tf_op jit(solution)/shard_map/ppermute | solution.py:12
Sparse Core Ops, SparseCore 0:
  10.0 77.5 all-gather.2

commit v2 on v1

v2 whole, which is shorter than its diff:
```python
import functools
import math

import jax
import jax.numpy as jnp
from jax import lax
from jax.experimental import pallas as pl
from jax.sharding import PartitionSpec as P


def from_behind(block, axis, distance):
    devices = range(lax.axis_size(axis))
    route = [((i - distance) % len(devices), i) for i in devices]
    return lax.ppermute(block, axis, route)


def bound_of(segments, limits):
    levels = jnp.arange(limits.shape[0])
    return jnp.sum(jnp.where(segments[:, None] == levels[None, :], limits[None, :], 0), axis=1)


def attention_kernel(q_ref, g_ref, b_ref, o_ref, *, groups, head_size, scale):
    h = pl.program_id(0)
    parts = g_ref.shape[0]
    span = parts * head_size
    k_at = pl.multiple_of(h * 2 * head_size, 2 * head_size)
    v_at = pl.multiple_of(h * 2 * head_size + head_size, head_size)
    k = g_ref[:, pl.ds(k_at, head_size), :].reshape(span, head_size)
    v = g_ref[:, pl.ds(v_at, head_size), :].reshape(span, head_size)
    bias = b_ref[...]
    for g in range(groups):
        qg = q_ref[:, g * head_size : (g + 1) * head_size]
        s = lax.dot_general(qg, k, (((1,), (1,)), ((), ())), preferred_element_type=jnp.float32)
        s = s * scale + bias
        m = jnp.max(s, axis=1, keepdims=True)
        w = jnp.exp(s - m)
        total = jnp.sum(w, axis=1, keepdims=True)
        pv = jnp.dot(w.astype(jnp.bfloat16), v, preferred_element_type=jnp.float32)
        o_ref[:, g * head_size : (g + 1) * head_size] = (pv / total).astype(o_ref.dtype)


def attention(q, gathered, bias, kv_heads, head_size):
    rows, width = q.shape
    groups = width // head_size // kv_heads
    block = groups * head_size
    kernel = functools.partial(
        attention_kernel, groups=groups, head_size=head_size, scale=1.0 / math.sqrt(head_size)
    )
    return pl.pallas_call(
        kernel,
        grid=(kv_heads,),
        in_specs=[
            pl.BlockSpec((rows, block), lambda h: (0, h)),
            pl.BlockSpec(gathered.shape, lambda h: (0, 0, 0)),
            pl.BlockSpec(bias.shape, lambda h: (0, 0)),
        ],
        out_specs=pl.BlockSpec((rows, block), lambda h: (0, h)),
        out_shape=jax.ShapeDtypeStruct((rows, width), jnp.bfloat16),
    )(q, gathered, bias)


def shards(queries, keys_values, segment_ids, bounds):
    query_rows = queries[0]
    pairs = keys_values[0]
    segments = segment_ids[0]
    limits = bounds[0]
    rows = query_rows.shape[0]
    kv_heads = pairs.shape[1]
    width = pairs.shape[2]
    head_size = width // 2
    lane = 128
    levels = limits.shape[0]
    tensor_size = lax.axis_size("tensor")

    body = pairs.reshape(rows, kv_heads, 2, head_size).transpose(1, 2, 0, 3).reshape(-1, head_size)
    extra = jnp.zeros((16, lane), jnp.bfloat16)
    extra = extra.at[0, :rows].set(segments.astype(jnp.bfloat16))
    extra = extra.at[1, :levels].set((limits // 32).astype(jnp.bfloat16))
    extra = extra.at[1, levels : 2 * levels].set((limits % 32).astype(jnp.bfloat16))
    packed = jnp.concatenate([body, extra], axis=0)
    body_rows = body.shape[0]

    packed_prev = from_behind(packed, "section", 1)
    query_prev = from_behind(query_rows, "section", 1)
    gathered = lax.all_gather(packed_prev, "tensor", axis=0, tiled=False)

    key_segment = gathered[:, body_rows, :rows].reshape(tensor_size * rows).astype(jnp.int32)
    own_segment = packed_prev[body_rows, :rows].astype(jnp.int32)
    halves = packed_prev[body_rows + 1].astype(jnp.int32)
    limits_prev = halves[:levels] * 32 + halves[levels : 2 * levels]

    my_first = lax.axis_index("tensor") * rows
    query_pos = my_first + jnp.arange(rows)
    query_bound = bound_of(own_segment, limits_prev)
    key_pos = jnp.arange(tensor_size * rows)
    visible = (own_segment[:, None] == key_segment[None, :]) & (
        (key_pos[None, :] <= query_pos[:, None]) | (key_pos[None, :] <= query_bound[:, None])
    )
    mask_bias = jnp.where(visible, 0.0, -1e30).astype(jnp.float32)

    result = attention(query_prev, gathered, mask_bias, kv_heads, head_size)
    return result[None]


def solution(mesh):
    in_specs = (
        P("section", ("dp", "tensor"), None),
        P("section", ("dp", "tensor"), None, None),
        P("section", ("dp", "tensor")),
        P("section", "dp"),
    )
    out_specs = P("section", ("dp", "tensor"), None)
    return jax.shard_map(shards, mesh=mesh, in_specs=in_specs, out_specs=out_specs, check_vma=False)
```

time: 238 us -> 220 us (0.924)
  local copies, waits for them, and re-layouts: 20 us -> 3.21 us
  matrix products: 15.7 us -> 0 us
  Pallas kernels: 0 us -> 14.3 us
  other arithmetic: 10.2 us -> 4 us
  waiting for transfers between devices: 148 us -> 153 us
    all_gather x1, waiting for transfers between devices: 76.2 us -> 146 us  [shards(): gathered = lax.all_gather(packed_prev, 'tensor', axis=0, tiled=False)]
    ppermute x4 -> x2, waiting for transfers between devices: 72.2 us -> 6.99 us  [from_behind(): return lax.ppermute(block, axis, route)]
    dot_general x8 -> x0, matrix products: 15.7 us -> none  [the longest x4 8.5 us: attend(): jnp.einsum('grn,nd->grd', weight.astype(jnp.bfloat16), v_h, preferred_ele...]
    pallas_call x0 -> x1, Pallas kernels: none -> 14.3 us  [attention(): pl.pallas_call(kernel, grid=(kv_heads,), in_specs=[pl.BlockSpec((rows, bl...]
    slice x2 -> x0, local copies, waits for them, and re-layouts: 7.67 us -> none  [the longest x1 4.63 us: attend(): v_h = pair_piece[:, h, head_size:]]
    reduce_sum x1 -> x0, other arithmetic: 6.07 us -> none  [attend(): total = jnp.sum(weight, axis=-1)]
    unnamed x21 -> x4, local copies, waits for them, and re-layouts: 7.57 us -> 1.69 us
    reshape x1 -> x0, local copies, waits for them, and re-layouts: 3.15 us -> none  [attend(): gathered[:, :body_rows].reshape(tensor_size * rows, kv_heads, width)]
  transfers between devices with their start and end apart: 5 -> 3, of which waited for: 5 -> 2; matrix products, arithmetic and copies ran while one was open for 1% -> 1% of each run, Pallas kernels for 0% -> 0%
where the time goes in v2:
time: 220 us; the launch traced here: 219 us
  waiting for transfers between devices  153 us (70%)
  starting transfers between devices  31 us (14%)
  Pallas kernels  14.3 us (6%)
  between operations  13.5 us (6%)
  other arithmetic  4 us (2%)
  local copies, waits for them, and re-layouts  3.21 us (1%)
    all_gather x1, waiting for transfers between devices, shards(): gathered = lax.all_gather(packed_prev, 'tensor', axis=0, tiled=False)  146 us
    ppermute x2, starting transfers between devices, from_behind(): return lax.ppermute(block, axis, route)  31 us
    pallas_call x1, Pallas kernels, attention(): pl.pallas_call(kernel, grid=(kv_heads,), in_specs=[pl.BlockSpec((rows, bl...  14.3 us
    ppermute x2, waiting for transfers between devices, from_behind(): return lax.ppermute(block, axis, route)  6.99 us
  transfers between devices with their start and end apart: 3, of which 2 were waited for; matrix products, arithmetic and copies ran while one was open for 1% of the time, Pallas kernels for 0%

profile of v2, /device:TPU:1, one launch (start us, length us, event | category | flops | bytes accessed | tf_op | source)
XLA Modules:
  0.0 219.1 jit_solution(7648930993457447839)
XLA Ops:
  6.5 0.0 all-gather.3.cloned.1.call-start
  6.5 0.7 convert_element_type.36
  7.2 0.7 fusion.3
  7.9 1.1 reshape_squeeze.4
  9.0 0.2 scatter.11
  9.1 0.3 scatter.14
  9.4 19.9 %collective-permute-start.1 = (bf16[1040,128]{1,0:T(8,128)(2,1)S(1)}, bf16[1040,128]{1,0:T(8,128)(2,1)S(1)}, u32[]{:S(2)}, u32[]{:S(2)}) collective-permute-start(bf16[1040,128]{1,0:T(8,128)(2,1)S(1)} %pad_maximum_fusion), channel_id=1, source_target_pairs={{960,0},{0,64},{64,128},{128,192},{192,256},{256,320},{320,384},{3... | collective-permute-start | bytes 798728 | tf_op jit(solution)/shard_map/ppermute | solution.py:14
  29.4 7.0 %collective-permute-done.1 = bf16[1040,128]{1,0:T(8,128)(2,1)S(1)} collective-permute-done((bf16[1040,128]{1,0:T(8,128)(2,1)S(1)}, bf16[1040,128]{1,0:T(8,128)(2,1)S(1)}, u32[]{:S(2)}, u32[]{:S(2)}) %collective-permute-start.1) | collective-permute-done | bytes 266272 | tf_op jit(solution)/shard_map/ppermute | solution.py:14
  36.3 0.0 copy-start.1
  36.4 0.7 copy-done.1
  37.1 0.0 all-gather.3.cloned.1.call-update
  37.1 11.1 %collective-permute-start = (bf16[128,4096]{1,0:T(8,128)(2,1)}, bf16[128,4096]{1,0:T(8,128)(2,1)S(1)}, u32[]{:S(2)}, u32[]{:S(2)}) collective-permute-start(bf16[128,4096]{1,0:T(8,128)(2,1)} %bitcast.18), channel_id=1, source_target_pairs={{960,0},{0,64},{64,128},{128,192},{192,256},{256,320},{320,384},{3... | collective-permute-start | bytes 3145736 | tf_op jit(solution)/shard_map/ppermute | solution.py:14
  48.2 0.8 fusion.4
  49.0 0.1 add_bitcast_fusion
  49.1 0.1 select_reduce_fusion
  49.1 146.0 %all-gather.3.cloned.1.call-done = bf16[8320,128]{1,0:T(8,128)(2,1)} async-done(((bf16[1040,128]{1,0:T(8,128)(2,1)}), bf16[8320,128]{1,0:T(8,128)(2,1)}) %all-gather.3.cloned.1.call-update) | async-done | bytes 2129936 | tf_op jit(solution)/shard_map/all_gather | solution.py:85
  195.2 0.7 slice_convert_fusion
  195.9 1.0 fusion.2.b_ref
  196.9 0.0 collective-permute-done.q_ref
  196.9 0.0 copy-start
  196.9 1.0 copy-done
  197.9 14.3 %shard_map.46 = bf16[128,4096]{1,0:T(8,128)(2,1)} custom-call(bf16[128,4096]{1,0:T(8,128)(2,1)} %copy-done, bf16[8,1040,128]{2,1,0:T(8,128)(2,1)} %bitcast.15, f32[128,1024]{1,0:T(8,128)} %fusion.2.b_ref), custom_call_target="tpu_custom_call" | custom-call | tf_op jit(solution)/shard_map/pallas_call | solution.py:49
  (4 shorter events, 0.1 us)
Async XLA Ops:
  6.5 188.7 %all-gather.3.cloned.1.call-start = ((), (), s32[]{:S(2)}) async-start(), calls=%async_computation | async-start | bytes 2396160 | tf_op jit(solution)/shard_map/all_gather | solution.py:85
  9.4 26.9 %collective-permute-start.1 = (bf16[1040,128]{1,0:T(8,128)(2,1)S(1)}, bf16[1040,128]{1,0:T(8,128)(2,1)S(1)}, u32[]{:S(2)}, u32[]{:S(2)}) collective-permute-start(bf16[1040,128]{1,0:T(8,128)(2,1)S(1)} %pad_maximum_fusion), channel_id=1, source_target_pairs={{960,0},{0,64},{64,128},{128,192},{192,256},{256,320},{320,384},{3... | collective-permute-start | bytes 798728 | tf_op jit(solution)/shard_map/ppermute | solution.py:14
  36.3 0.7 copy-start.1
  37.1 159.8 %collective-permute-start = (bf16[128,4096]{1,0:T(8,128)(2,1)}, bf16[128,4096]{1,0:T(8,128)(2,1)S(1)}, u32[]{:S(2)}, u32[]{:S(2)}) collective-permute-start(bf16[128,4096]{1,0:T(8,128)(2,1)} %bitcast.18), channel_id=1, source_target_pairs={{960,0},{0,64},{64,128},{128,192},{192,256},{256,320},{320,384},{3... | collective-permute-start | bytes 3145736 | tf_op jit(solution)/shard_map/ppermute | solution.py:14
  196.9 1.0 copy-start
Sparse Core Ops, SparseCore 0:
  37.2 157.9 all-gather.2

commit v3 on v2

--- a/solution.py
+++ b/solution.py
@@ -19,14 +19,13 @@
     return jnp.sum(jnp.where(segments[:, None] == levels[None, :], limits[None, :], 0), axis=1)
 
 
-def attention_kernel(q_ref, g_ref, b_ref, o_ref, *, groups, head_size, scale):
+def attention_kernel(q_ref, *refs, groups, head_size, scale):
+    slot_refs, b_ref, o_ref = refs[:-2], refs[-2], refs[-1]
     h = pl.program_id(0)
-    parts = g_ref.shape[0]
-    span = parts * head_size
     k_at = pl.multiple_of(h * 2 * head_size, 2 * head_size)
     v_at = pl.multiple_of(h * 2 * head_size + head_size, head_size)
-    k = g_ref[:, pl.ds(k_at, head_size), :].reshape(span, head_size)
-    v = g_ref[:, pl.ds(v_at, head_size), :].reshape(span, head_size)
+    k = jnp.concatenate([r[pl.ds(k_at, head_size), :] for r in slot_refs], axis=0)
+    v = jnp.concatenate([r[pl.ds(v_at, head_size), :] for r in slot_refs], axis=0)
     bias = b_ref[...]
     for g in range(groups):
         qg = q_ref[:, g * head_size : (g + 1) * head_size]
@@ -39,7 +38,7 @@
         o_ref[:, g * head_size : (g + 1) * head_size] = (pv / total).astype(o_ref.dtype)
 
 
-def attention(q, gathered, bias, kv_heads, head_size):
+def attention(q, slots, bias, kv_heads, head_size):
     rows, width = q.shape
     groups = width // head_size // kv_heads
     block = groups * head_size
@@ -51,12 +50,21 @@
         grid=(kv_heads,),
         in_specs=[
             pl.BlockSpec((rows, block), lambda h: (0, h)),
-            pl.BlockSpec(gathered.shape, lambda h: (0, 0, 0)),
+            *[pl.BlockSpec(x.shape, lambda h: (0, 0)) for x in slots],
             pl.BlockSpec(bias.shape, lambda h: (0, 0)),
         ],
         out_specs=pl.BlockSpec((rows, block), lambda h: (0, h)),
         out_shape=jax.ShapeDtypeStruct((rows, width), jnp.bfloat16),
-    )(q, gathered, bias)
+    )(q, *slots, bias)
+
+
+def ring_gather(x, axis):
+    n = lax.axis_size(axis)
+    route = [(i, (i + 1) % n) for i in range(n)]
+    slots = [x]
+    for k in range(1, n):
+        slots.append(lax.ppermute(slots[-1], axis, route))
+    return slots
 
 
 def shards(queries, keys_values, segment_ids, bounds):
@@ -82,9 +90,9 @@
 
     packed_prev = from_behind(packed, "section", 1)
     query_prev = from_behind(query_rows, "section", 1)
-    gathered = lax.all_gather(packed_prev, "tensor", axis=0, tiled=False)
+    slots = ring_gather(packed_prev, "tensor")
 
-    key_segment = gathered[:, body_rows, :rows].reshape(tensor_size * rows).astype(jnp.int32)
+    key_segment = jnp.concatenate([x[body_rows, :rows] for x in slots]).astype(jnp.int32)
     own_segment = packed_prev[body_rows, :rows].astype(jnp.int32)
     halves = packed_prev[body_rows + 1].astype(jnp.int32)
     limits_prev = halves[:levels] * 32 + halves[levels : 2 * levels]
@@ -92,13 +100,14 @@
     my_first = lax.axis_index("tensor") * rows
     query_pos = my_first + jnp.arange(rows)
     query_bound = bound_of(own_segment, limits_prev)
-    key_pos = jnp.arange(tensor_size * rows)
+    me = lax.axis_index("tensor")
+    key_pos = jnp.concatenate([((me - k) % tensor_size) * rows + jnp.arange(rows) for k in range(tensor_size)])
     visible = (own_segment[:, None] == key_segment[None, :]) & (
         (key_pos[None, :] <= query_pos[:, None]) | (key_pos[None, :] <= query_bound[:, None])
     )
     mask_bias = jnp.where(visible, 0.0, -1e30).astype(jnp.float32)
 
-    result = attention(query_prev, gathered, mask_bias, kv_heads, head_size)
+    result = attention(query_prev, slots, mask_bias, kv_heads, head_size)
     return result[None]
 
 

time: 220 us -> 250 us (1.14)
  the two profiles are of different devices: /device:TPU:1 before, /device:TPU:18 now
where the time goes in v3:
time: 250 us
  waiting for transfers between devices  172 us (69%)
  starting transfers between devices  56.9 us (23%)
  Pallas kernels  14.4 us (6%)
  local copies, waits for them, and re-layouts  4.25 us (2%)
    ppermute x7, waiting for transfers between devices, ring_gather(): slots.append(lax.ppermute(slots[-1], axis, route))  160 us
    ppermute x7, starting transfers between devices, ring_gather(): slots.append(lax.ppermute(slots[-1], axis, route))  35.6 us
    ppermute x2, starting transfers between devices, from_behind(): return lax.ppermute(block, axis, route)  21.3 us
    pallas_call x1, Pallas kernels, attention(): pl.pallas_call(kernel, grid=(kv_heads,), in_specs=[pl.BlockSpec((rows, bl...  14.4 us
    ppermute x2, waiting for transfers between devices, from_behind(): return lax.ppermute(block, axis, route)  12.1 us
  transfers between devices with their start and end apart: 9, of which 8 were waited for; matrix products, arithmetic and copies ran while one was open for 1% of the time, Pallas kernels for 0%

profile of v3, /device:TPU:18, one launch (start us, length us, event | category | flops | bytes accessed | tf_op | source)
XLA Modules:
  0.0 249.7 jit_solution(16802516671589865480)
XLA Ops:
  0.0 0.7 convert_element_type.30
  0.7 1.1 reshape_squeeze.3
  1.8 0.2 scatter.11
  2.0 0.3 scatter.14
  2.3 19.4 %collective-permute-start.1 = (bf16[1040,128]{1,0:T(8,128)(2,1)S(1)}, bf16[1040,128]{1,0:T(8,128)(2,1)S(1)}, u32[]{:S(2)}, u32[]{:S(2)}) collective-permute-start(bf16[1040,128]{1,0:T(8,128)(2,1)S(1)} %pad_maximum_fusion), channel_id=1, source_target_pairs={{960,0},{0,64},{64,128},{128,192},{192,256},{256,320},{320,384},{3... | collective-permute-start | bytes 798728 | tf_op jit(solution)/shard_map/ppermute | solution.py:14
  21.6 1.9 collective-permute-start
  23.6 12.1 %collective-permute-done.1.refs_0_ = bf16[1040,128]{1,0:T(8,128)(2,1)S(1)} collective-permute-done((bf16[1040,128]{1,0:T(8,128)(2,1)S(1)}, bf16[1040,128]{1,0:T(8,128)(2,1)S(1)}, u32[]{:S(2)}, u32[]{:S(2)}) %collective-permute-start.1) | collective-permute-done | bytes 266272 | tf_op jit(solution)/shard_map/ppermute | solution.py:14
  35.8 21.7 %collective-permute-start.2 = (bf16[1040,128]{1,0:T(8,128)(2,1)S(1)}, bf16[1040,128]{1,0:T(8,128)(2,1)S(1)}, u32[]{:S(2)}, u32[]{:S(2)}) collective-permute-start(bf16[1040,128]{1,0:T(8,128)(2,1)S(1)} %collective-permute-done.1.refs_0_), channel_id=1, source_target_pairs={{0,1},{1,2},{2,3},{3,4},{4,5},{5,6},{6,7},{7,0},{8,9},{9,10},{10,1... | collective-permute-start | bytes 798728 | tf_op jit(solution)/shard_map/ppermute | solution.py:66
  57.6 81.2 %collective-permute-done.2.refs_1_ = bf16[1040,128]{1,0:T(8,128)(2,1)S(1)} collective-permute-done((bf16[1040,128]{1,0:T(8,128)(2,1)S(1)}, bf16[1040,128]{1,0:T(8,128)(2,1)S(1)}, u32[]{:S(2)}, u32[]{:S(2)}) %collective-permute-start.2) | collective-permute-done | bytes 266272 | tf_op jit(solution)/shard_map/ppermute | solution.py:66
  138.8 4.4 %collective-permute-start.3 = (bf16[1040,128]{1,0:T(8,128)(2,1)S(1)}, bf16[1040,128]{1,0:T(8,128)(2,1)S(1)}, u32[]{:S(2)}, u32[]{:S(2)}) collective-permute-start(bf16[1040,128]{1,0:T(8,128)(2,1)S(1)} %collective-permute-done.2.refs_1_), channel_id=1, source_target_pairs={{0,1},{1,2},{2,3},{3,4},{4,5},{5,6},{6,7},{7,0},{8,9},{9,10},{10,1... | collective-permute-start | bytes 798728 | tf_op jit(solution)/shard_map/ppermute | solution.py:66
  143.3 13.5 %collective-permute-done.3.refs_2_ = bf16[1040,128]{1,0:T(8,128)(2,1)S(1)} collective-permute-done((bf16[1040,128]{1,0:T(8,128)(2,1)S(1)}, bf16[1040,128]{1,0:T(8,128)(2,1)S(1)}, u32[]{:S(2)}, u32[]{:S(2)}) %collective-permute-start.3) | collective-permute-done | bytes 266272 | tf_op jit(solution)/shard_map/ppermute | solution.py:66
  156.7 1.9 collective-permute-start.4
  158.7 0.2 dynamic-update-slice.15
  158.9 14.0 %collective-permute-done.4.refs_3_ = bf16[1040,128]{1,0:T(8,128)(2,1)S(1)} collective-permute-done((bf16[1040,128]{1,0:T(8,128)(2,1)S(1)}, bf16[1040,128]{1,0:T(8,128)(2,1)S(1)}, u32[]{:S(2)}, u32[]{:S(2)}) %collective-permute-start.4) | collective-permute-done | bytes 266272 | tf_op jit(solution)/shard_map/ppermute | solution.py:66
  173.0 1.9 collective-permute-start.5
  175.1 13.3 %collective-permute-done.5.refs_4_ = bf16[1040,128]{1,0:T(8,128)(2,1)S(1)} collective-permute-done((bf16[1040,128]{1,0:T(8,128)(2,1)S(1)}, bf16[1040,128]{1,0:T(8,128)(2,1)S(1)}, u32[]{:S(2)}, u32[]{:S(2)}) %collective-permute-start.5) | collective-permute-done | bytes 266272 | tf_op jit(solution)/shard_map/ppermute | solution.py:66
  188.3 1.9 collective-permute-start.6
  190.3 0.2 dynamic-update-slice.16
  190.5 0.2 dynamic-update-slice.17
  190.7 12.5 %collective-permute-done.6.refs_5_ = bf16[1040,128]{1,0:T(8,128)(2,1)S(1)} collective-permute-done((bf16[1040,128]{1,0:T(8,128)(2,1)S(1)}, bf16[1040,128]{1,0:T(8,128)(2,1)S(1)}, u32[]{:S(2)}, u32[]{:S(2)}) %collective-permute-start.6) | collective-permute-done | bytes 266272 | tf_op jit(solution)/shard_map/ppermute | solution.py:66
  203.3 1.9 collective-permute-start.7
  205.2 0.2 dynamic-update-slice.18
  205.4 0.2 dynamic-update-slice.19
  205.6 12.5 %collective-permute-done.7.refs_6_ = bf16[1040,128]{1,0:T(8,128)(2,1)S(1)} collective-permute-done((bf16[1040,128]{1,0:T(8,128)(2,1)S(1)}, bf16[1040,128]{1,0:T(8,128)(2,1)S(1)}, u32[]{:S(2)}, u32[]{:S(2)}) %collective-permute-start.7) | collective-permute-done | bytes 266272 | tf_op jit(solution)/shard_map/ppermute | solution.py:66
  218.2 1.9 collective-permute-start.8
  220.1 0.2 dynamic-update-slice.20
  220.3 0.2 dynamic-update-slice.21
  220.5 12.5 %collective-permute-done.8.refs_7_ = bf16[1040,128]{1,0:T(8,128)(2,1)S(1)} collective-permute-done((bf16[1040,128]{1,0:T(8,128)(2,1)S(1)}, bf16[1040,128]{1,0:T(8,128)(2,1)S(1)}, u32[]{:S(2)}, u32[]{:S(2)}) %collective-permute-start.8) | collective-permute-done | bytes 266272 | tf_op jit(solution)/shard_map/ppermute | solution.py:66
  233.1 0.2 dynamic-update-slice.22
  233.2 1.0 and_select_fusion.refs_8_
  234.3 1.0 copy-done
  235.3 14.4 %shard_map.46 = bf16[128,4096]{1,0:T(8,128)(2,1)} custom-call(bf16[128,4096]{1,0:T(8,128)(2,1)} %copy-done, bf16[1040,128]{1,0:T(8,128)(2,1)} %copy-done.1, bf16[1040,128]{1,0:T(8,128)(2,1)} %copy-done.2, bf16[1040,128]{1,0:T(8,128)(2,1)} %copy-done.3, bf16[1040,128]{1,0:T(8,128)(2,1)} %copy-done.4, bf16[1040,128]{1,0:T(8,128)(2,1)} %copy-done.5, ...), custom_call_target="tpu_custom_call" | custom-call | tf_op jit(solution)/shard_map/pallas_call | solution.py:48
  (45 shorter events, 0.4 us)
Async XLA Ops:
  0.0 0.7 copy-start.9
  2.3 33.5 %collective-permute-start.1 = (bf16[1040,128]{1,0:T(8,128)(2,1)S(1)}, bf16[1040,128]{1,0:T(8,128)(2,1)S(1)}, u32[]{:S(2)}, u32[]{:S(2)}) collective-permute-start(bf16[1040,128]{1,0:T(8,128)(2,1)S(1)} %pad_maximum_fusion), channel_id=1, source_target_pairs={{960,0},{0,64},{64,128},{128,192},{192,256},{256,320},{320,384},{3... | collective-permute-start | bytes 798728 | tf_op jit(solution)/shard_map/ppermute | solution.py:14
  21.6 212.6 %collective-permute-start = (bf16[128,4096]{1,0:T(8,128)(2,1)}, bf16[128,4096]{1,0:T(8,128)(2,1)S(1)}, u32[]{:S(2)}, u32[]{:S(2)}) collective-permute-start(bf16[128,4096]{1,0:T(8,128)(2,1)} %bitcast), channel_id=1, source_target_pairs={{960,0},{0,64},{64,128},{128,192},{192,256},{256,320},{320,384},{3... | collective-permute-start | bytes 3145736 | tf_op jit(solution)/shard_map/ppermute | solution.py:14
  35.8 198.4 %copy-start.1 = (bf16[1040,128]{1,0:T(8,128)(2,1)}, bf16[1040,128]{1,0:T(8,128)(2,1)S(1)}, u32[]{:S(2)}) copy-start(bf16[1040,128]{1,0:T(8,128)(2,1)S(1)} %collective-permute-done.1.refs_0_) | copy-start | bytes 798724
  35.8 103.0 %collective-permute-start.2 = (bf16[1040,128]{1,0:T(8,128)(2,1)S(1)}, bf16[1040,128]{1,0:T(8,128)(2,1)S(1)}, u32[]{:S(2)}, u32[]{:S(2)}) collective-permute-start(bf16[1040,128]{1,0:T(8,128)(2,1)S(1)} %collective-permute-done.1.refs_0_), channel_id=1, source_target_pairs={{0,1},{1,2},{2,3},{3,4},{4,5},{5,6},{6,7},{7,0},{8,9},{9,10},{10,1... | collective-permute-start | bytes 798728 | tf_op jit(solution)/shard_map/ppermute | solution.py:66
  138.8 95.4 %copy-start.2 = (bf16[1040,128]{1,0:T(8,128)(2,1)}, bf16[1040,128]{1,0:T(8,128)(2,1)S(1)}, u32[]{:S(2)}) copy-start(bf16[1040,128]{1,0:T(8,128)(2,1)S(1)} %collective-permute-done.2.refs_1_) | copy-start | bytes 798724
  138.8 18.0 %collective-permute-start.3 = (bf16[1040,128]{1,0:T(8,128)(2,1)S(1)}, bf16[1040,128]{1,0:T(8,128)(2,1)S(1)}, u32[]{:S(2)}, u32[]{:S(2)}) collective-permute-start(bf16[1040,128]{1,0:T(8,128)(2,1)S(1)} %collective-permute-done.2.refs_1_), channel_id=1, source_target_pairs={{0,1},{1,2},{2,3},{3,4},{4,5},{5,6},{6,7},{7,0},{8,9},{9,10},{10,1... | collective-permute-start | bytes 798728 | tf_op jit(solution)/shard_map/ppermute | solution.py:66
  156.7 77.5 %copy-start.3 = (bf16[1040,128]{1,0:T(8,128)(2,1)}, bf16[1040,128]{1,0:T(8,128)(2,1)S(1)}, u32[]{:S(2)}) copy-start(bf16[1040,128]{1,0:T(8,128)(2,1)S(1)} %collective-permute-done.3.refs_2_) | copy-start | bytes 798724
  156.7 16.2 %collective-permute-start.4 = (bf16[1040,128]{1,0:T(8,128)(2,1)S(1)}, bf16[1040,128]{1,0:T(8,128)(2,1)S(1)}, u32[]{:S(2)}, u32[]{:S(2)}) collective-permute-start(bf16[1040,128]{1,0:T(8,128)(2,1)S(1)} %collective-permute-done.3.refs_2_), channel_id=1, source_target_pairs={{0,1},{1,2},{2,3},{3,4},{4,5},{5,6},{6,7},{7,0},{8,9},{9,10},{10,1... | collective-permute-start | bytes 798728 | tf_op jit(solution)/shard_map/ppermute | solution.py:66
  173.0 61.3 %copy-start.4 = (bf16[1040,128]{1,0:T(8,128)(2,1)}, bf16[1040,128]{1,0:T(8,128)(2,1)S(1)}, u32[]{:S(2)}) copy-start(bf16[1040,128]{1,0:T(8,128)(2,1)S(1)} %collective-permute-done.4.refs_3_) | copy-start | bytes 798724
  173.0 15.4 %collective-permute-start.5 = (bf16[1040,128]{1,0:T(8,128)(2,1)S(1)}, bf16[1040,128]{1,0:T(8,128)(2,1)S(1)}, u32[]{:S(2)}, u32[]{:S(2)}) collective-permute-start(bf16[1040,128]{1,0:T(8,128)(2,1)S(1)} %collective-permute-done.4.refs_3_), channel_id=1, source_target_pairs={{0,1},{1,2},{2,3},{3,4},{4,5},{5,6},{6,7},{7,0},{8,9},{9,10},{10,1... | collective-permute-start | bytes 798728 | tf_op jit(solution)/shard_map/ppermute | solution.py:66
  188.3 45.9 %copy-start.5 = (bf16[1040,128]{1,0:T(8,128)(2,1)}, bf16[1040,128]{1,0:T(8,128)(2,1)S(1)}, u32[]{:S(2)}) copy-start(bf16[1040,128]{1,0:T(8,128)(2,1)S(1)} %collective-permute-done.5.refs_4_) | copy-start | bytes 798724
  188.3 14.9 %collective-permute-start.6 = (bf16[1040,128]{1,0:T(8,128)(2,1)S(1)}, bf16[1040,128]{1,0:T(8,128)(2,1)S(1)}, u32[]{:S(2)}, u32[]{:S(2)}) collective-permute-start(bf16[1040,128]{1,0:T(8,128)(2,1)S(1)} %collective-permute-done.5.refs_4_), channel_id=1, source_target_pairs={{0,1},{1,2},{2,3},{3,4},{4,5},{5,6},{6,7},{7,0},{8,9},{9,10},{10,1... | collective-permute-start | bytes 798728 | tf_op jit(solution)/shard_map/ppermute | solution.py:66
  203.2 31.0 %copy-start.6 = (bf16[1040,128]{1,0:T(8,128)(2,1)}, bf16[1040,128]{1,0:T(8,128)(2,1)S(1)}, u32[]{:S(2)}) copy-start(bf16[1040,128]{1,0:T(8,128)(2,1)S(1)} %collective-permute-done.6.refs_5_) | copy-start | bytes 798724
  203.3 14.9 %collective-permute-start.7 = (bf16[1040,128]{1,0:T(8,128)(2,1)S(1)}, bf16[1040,128]{1,0:T(8,128)(2,1)S(1)}, u32[]{:S(2)}, u32[]{:S(2)}) collective-permute-start(bf16[1040,128]{1,0:T(8,128)(2,1)S(1)} %collective-permute-done.6.refs_5_), channel_id=1, source_target_pairs={{0,1},{1,2},{2,3},{3,4},{4,5},{5,6},{6,7},{7,0},{8,9},{9,10},{10,1... | collective-permute-start | bytes 798728 | tf_op jit(solution)/shard_map/ppermute | solution.py:66
  218.2 16.1 %copy-start.7 = (bf16[1040,128]{1,0:T(8,128)(2,1)}, bf16[1040,128]{1,0:T(8,128)(2,1)S(1)}, u32[]{:S(2)}) copy-start(bf16[1040,128]{1,0:T(8,128)(2,1)S(1)} %collective-permute-done.7.refs_6_) | copy-start | bytes 798724
  218.2 14.9 %collective-permute-start.8 = (bf16[1040,128]{1,0:T(8,128)(2,1)S(1)}, bf16[1040,128]{1,0:T(8,128)(2,1)S(1)}, u32[]{:S(2)}, u32[]{:S(2)}) collective-permute-start(bf16[1040,128]{1,0:T(8,128)(2,1)S(1)} %collective-permute-done.7.refs_6_), channel_id=1, source_target_pairs={{0,1},{1,2},{2,3},{3,4},{4,5},{5,6},{6,7},{7,0},{8,9},{9,10},{10,1... | collective-permute-start | bytes 798728 | tf_op jit(solution)/shard_map/ppermute | solution.py:66
  233.1 1.2 copy-start.8
  234.3 1.0 copy-start

commit v4 on v2

v4 whole, which is shorter than its diff:
```python
import functools
import math

import jax
import jax.numpy as jnp
from jax import lax
from jax.experimental import pallas as pl
from jax.sharding import PartitionSpec as P


def from_behind(block, axis, distance):
    devices = range(lax.axis_size(axis))
    route = [((i - distance) % len(devices), i) for i in devices]
    return lax.ppermute(block, axis, route)


def bound_of(segments, limits):
    levels = jnp.arange(limits.shape[0])
    return jnp.sum(jnp.where(segments[:, None] == levels[None, :], limits[None, :], 0), axis=1)


def attention_kernel(q_ref, g_ref, b_ref, o_ref, *, head, groups, head_size, scale):
    parts = g_ref.shape[0]
    span = parts * head_size
    k_at = head * 2 * head_size
    k = g_ref[:, k_at : k_at + head_size, :].reshape(span, head_size)
    v = g_ref[:, k_at + head_size : k_at + 2 * head_size, :].reshape(span, head_size)
    bias = b_ref[...]
    for g in range(groups):
        qg = q_ref[:, g * head_size : (g + 1) * head_size]
        s = lax.dot_general(qg, k, (((1,), (1,)), ((), ())), preferred_element_type=jnp.float32)
        s = s * scale + bias
        m = jnp.max(s, axis=1, keepdims=True)
        w = jnp.exp(s - m)
        total = jnp.sum(w, axis=1, keepdims=True)
        pv = jnp.dot(w.astype(jnp.bfloat16), v, preferred_element_type=jnp.float32)
        o_ref[:, g * head_size : (g + 1) * head_size] = (pv / total).astype(o_ref.dtype)


def attention_head(q, gathered, bias, head, kv_heads, head_size):
    rows, width = q.shape
    groups = width // head_size // kv_heads
    block = groups * head_size
    kernel = functools.partial(
        attention_kernel, head=head, groups=groups, head_size=head_size, scale=1.0 / math.sqrt(head_size)
    )
    return pl.pallas_call(
        kernel,
        grid=(1,),
        in_specs=[
            pl.BlockSpec((rows, block), lambda i: (0, head)),
            pl.BlockSpec(gathered.shape, lambda i: (0, 0, 0)),
            pl.BlockSpec(bias.shape, lambda i: (0, 0)),
        ],
        out_specs=pl.BlockSpec((rows, block), lambda i: (0, 0)),
        out_shape=jax.ShapeDtypeStruct((rows, block), jnp.bfloat16),
    )(q, gathered, bias)


def attend(queries, keys_values, segment_ids, bounds):
    query_rows = queries[0]
    pairs = keys_values[0]
    segments = segment_ids[0]
    limits = bounds[0]
    rows = query_rows.shape[0]
    kv_heads = pairs.shape[1]
    width = pairs.shape[2]
    head_size = width // 2
    lane = 128
    tensor_size = lax.axis_size("tensor")

    body = pairs.reshape(rows, kv_heads, 2, head_size).transpose(1, 2, 0, 3).reshape(-1, head_size)
    extra = jnp.zeros((16, lane), jnp.bfloat16)
    extra = extra.at[0, :rows].set(segments.astype(jnp.bfloat16))
    packed = jnp.concatenate([body, extra], axis=0)
    body_rows = body.shape[0]
    gathered = lax.all_gather(packed, "tensor", axis=0, tiled=False)
    key_segment = gathered[:, body_rows, :rows].reshape(tensor_size * rows).astype(jnp.int32)

    my_first = lax.axis_index("tensor") * rows
    query_pos = my_first + jnp.arange(rows)
    query_bound = bound_of(segments, limits)
    key_pos = jnp.arange(tensor_size * rows)
    visible = (segments[:, None] == key_segment[None, :]) & (
        (key_pos[None, :] <= query_pos[:, None]) | (key_pos[None, :] <= query_bound[:, None])
    )
    mask_bias = jnp.where(visible, 0.0, -1e30).astype(jnp.float32)

    pieces = []
    for h in range(kv_heads):
        out_h = attention_head(query_rows, gathered, mask_bias, h, kv_heads, head_size)
        pieces.append(from_behind(out_h, "section", 1))
    return jnp.concatenate(pieces, axis=1)[None]


def solution(mesh):
    in_specs = (
        P("section", ("dp", "tensor"), None),
        P("section", ("dp", "tensor"), None, None),
        P("section", ("dp", "tensor")),
        P("section", "dp"),
    )
    out_specs = P("section", ("dp", "tensor"), None)
    return jax.shard_map(attend, mesh=mesh, in_specs=in_specs, out_specs=out_specs, check_vma=False)
```

time: 220 us -> 222 us (level)
  Pallas kernels: 14.3 us -> 21.7 us
  waiting for transfers between devices: 153 us -> 150 us
    all_gather x1, waiting for transfers between devices: 146 us -> 77.8 us  [attend(): gathered = lax.all_gather(packed, 'tensor', axis=0, tiled=False)]
    ppermute x2 -> x4, waiting for transfers between devices: 6.99 us -> 72.4 us  [from_behind(): return lax.ppermute(block, axis, route)]
    pallas_call x1 -> x4, Pallas kernels: 14.3 us -> 21.7 us  [attention_head(): pl.pallas_call(kernel, grid=(1,), in_specs=[pl.BlockSpec((rows, block), l...]
    ppermute x2 -> x4, starting transfers between devices: 31 us -> 29.7 us  [from_behind(): return lax.ppermute(block, axis, route)]
  transfers between devices with their start and end apart: 3 -> 5, of which waited for: 2 -> 5; matrix products, arithmetic and copies ran while one was open for 1% -> 0% of each run, Pallas kernels for 0% -> 0%
where the time goes in v4:
time: 222 us
  waiting for transfers between devices  150 us (68%)
  starting transfers between devices  29.7 us (13%)
  Pallas kernels  21.7 us (10%)
  between operations  13.5 us (6%)
  other arithmetic  5.56 us (3%)
    all_gather x1, waiting for transfers between devices, attend(): gathered = lax.all_gather(packed, 'tensor', axis=0, tiled=False)  77.8 us
    ppermute x4, waiting for transfers between devices, from_behind(): return lax.ppermute(block, axis, route)  72.4 us
    ppermute x4, starting transfers between devices, from_behind(): return lax.ppermute(block, axis, route)  29.7 us
    pallas_call x4, Pallas kernels, attention_head(): pl.pallas_call(kernel, grid=(1,), in_specs=[pl.BlockSpec((rows, block), l...  21.7 us
  transfers between devices with their start and end apart: 5, of which 5 were waited for; matrix products, arithmetic and copies ran while one was open for 0% of the time, Pallas kernels for 0%

profile of v4, /device:TPU:1, one launch (start us, length us, event | category | flops | bytes accessed | tf_op | source)
XLA Modules:
  0.0 221.6 jit_solution(7205173407586890516)
XLA Ops:
  6.5 0.0 all-gather.3.cloned.1.call-start
  6.5 0.7 convert_element_type.14
  7.2 1.1 reshape_squeeze.4
  8.3 0.7 fusion.4
  9.0 0.0 all-gather.3.cloned.1.call-update
  9.1 0.8 select_reduce_fusion
  9.8 77.8 %all-gather.3.cloned.1.call-done = bf16[8320,128]{1,0:T(8,128)(2,1)} async-done(((bf16[1040,128]{1,0:T(8,128)(2,1)}), bf16[8320,128]{1,0:T(8,128)(2,1)}) %all-gather.3.cloned.1.call-update) | async-done | bytes 2129936 | tf_op jit(solution)/shard_map/all_gather | solution.py:77
  87.6 0.7 slice_convert_fusion
  88.3 1.7 fusion.3.b_ref
  90.0 5.4 %shard_map.49 = bf16[128,1024]{1,0:T(8,128)(2,1)} custom-call(bf16[128,4096]{1,0:T(8,128)(2,1)} %bitcast.14, bf16[8,1040,128]{2,1,0:T(8,128)(2,1)} %bitcast.10, f32[128,1024]{1,0:T(8,128)} %fusion.3.b_ref), custom_call_target="tpu_custom_call" | custom-call | tf_op jit(solution)/shard_map/pallas_call | solution.py:47
  95.4 5.4 %shard_map.48 = bf16[128,1024]{1,0:T(8,128)(2,1)} custom-call(bf16[128,4096]{1,0:T(8,128)(2,1)} %bitcast.15, bf16[8,1040,128]{2,1,0:T(8,128)(2,1)} %bitcast.11, f32[128,1024]{1,0:T(8,128)} %fusion.3.b_ref), custom_call_target="tpu_custom_call" | custom-call | tf_op jit(solution)/shard_map/pallas_call | solution.py:47
  100.8 5.4 %shard_map.47 = bf16[128,1024]{1,0:T(8,128)(2,1)} custom-call(bf16[128,4096]{1,0:T(8,128)(2,1)} %bitcast.16, bf16[8,1040,128]{2,1,0:T(8,128)(2,1)} %bitcast.12, f32[128,1024]{1,0:T(8,128)} %fusion.3.b_ref), custom_call_target="tpu_custom_call" | custom-call | tf_op jit(solution)/shard_map/pallas_call | solution.py:47
  106.2 0.0 copy-start.2
  106.2 0.0 copy-start.1
  106.2 0.0 copy-start
  106.2 5.5 %shard_map.46 = bf16[128,1024]{1,0:T(8,128)(2,1)} custom-call(bf16[128,4096]{1,0:T(8,128)(2,1)} %bitcast.17, bf16[8,1040,128]{2,1,0:T(8,128)(2,1)} %bitcast.13, f32[128,1024]{1,0:T(8,128)} %fusion.3.b_ref), custom_call_target="tpu_custom_call" | custom-call | tf_op jit(solution)/shard_map/pallas_call | solution.py:47
  111.7 8.7 %collective-permute-start = (bf16[128,1024]{1,0:T(8,128)(2,1)}, bf16[128,1024]{1,0:T(8,128)(2,1)S(1)}, u32[]{:S(2)}, u32[]{:S(2)}) collective-permute-start(bf16[128,1024]{1,0:T(8,128)(2,1)} %shard_map.46), channel_id=1, source_target_pairs={{960,0},{0,64},{64,128},{128,192},{192,256},{256,320},{320,384},{3... | collective-permute-start | bytes 786440 | tf_op jit(solution)/shard_map/ppermute | solution.py:14
  120.4 0.0 copy-done.2
  120.4 6.0 %collective-permute-start.1 = (bf16[128,1024]{1,0:T(8,128)(2,1)S(1)}, bf16[128,1024]{1,0:T(8,128)(2,1)S(1)}, u32[]{:S(2)}, u32[]{:S(2)}) collective-permute-start(bf16[128,1024]{1,0:T(8,128)(2,1)S(1)} %copy-done.2), channel_id=1, source_target_pairs={{960,0},{0,64},{64,128},{128,192},{192,256},{256,320},{320,384},{3... | collective-permute-start | bytes 786440 | tf_op jit(solution)/shard_map/ppermute | solution.py:14
  126.5 0.0 copy-done.1
  126.5 8.9 %collective-permute-start.2 = (bf16[128,1024]{1,0:T(8,128)(2,1)S(1)}, bf16[128,1024]{1,0:T(8,128)(2,1)S(1)}, u32[]{:S(2)}, u32[]{:S(2)}) collective-permute-start(bf16[128,1024]{1,0:T(8,128)(2,1)S(1)} %copy-done.1), channel_id=1, source_target_pairs={{960,0},{0,64},{64,128},{128,192},{192,256},{256,320},{320,384},{3... | collective-permute-start | bytes 786440 | tf_op jit(solution)/shard_map/ppermute | solution.py:14
  135.4 0.0 copy-done
  135.4 6.0 %collective-permute-start.3 = (bf16[128,1024]{1,0:T(8,128)(2,1)S(1)}, bf16[128,1024]{1,0:T(8,128)(2,1)S(1)}, u32[]{:S(2)}, u32[]{:S(2)}) collective-permute-start(bf16[128,1024]{1,0:T(8,128)(2,1)S(1)} %copy-done), channel_id=1, source_target_pairs={{960,0},{0,64},{64,128},{128,192},{192,256},{256,320},{320,384},{3... | collective-permute-start | bytes 786440 | tf_op jit(solution)/shard_map/ppermute | solution.py:14
  141.4 46.9 %collective-permute-done = bf16[128,1024]{1,0:T(8,128)(2,1)S(1)} collective-permute-done((bf16[128,1024]{1,0:T(8,128)(2,1)}, bf16[128,1024]{1,0:T(8,128)(2,1)S(1)}, u32[]{:S(2)}, u32[]{:S(2)}) %collective-permute-start) | collective-permute-done | bytes 262176 | tf_op jit(solution)/shard_map/ppermute | solution.py:14
  188.3 14.3 %collective-permute-done.1 = bf16[128,1024]{1,0:T(8,128)(2,1)S(1)} collective-permute-done((bf16[128,1024]{1,0:T(8,128)(2,1)S(1)}, bf16[128,1024]{1,0:T(8,128)(2,1)S(1)}, u32[]{:S(2)}, u32[]{:S(2)}) %collective-permute-start.1) | collective-permute-done | bytes 262176 | tf_op jit(solution)/shard_map/ppermute | solution.py:14
  202.5 5.6 %collective-permute-done.2 = bf16[128,1024]{1,0:T(8,128)(2,1)S(1)} collective-permute-done((bf16[128,1024]{1,0:T(8,128)(2,1)S(1)}, bf16[128,1024]{1,0:T(8,128)(2,1)S(1)}, u32[]{:S(2)}, u32[]{:S(2)}) %collective-permute-start.2) | collective-permute-done | bytes 262176 | tf_op jit(solution)/shard_map/ppermute | solution.py:14
  208.1 5.6 %collective-permute-done.3 = bf16[128,1024]{1,0:T(8,128)(2,1)S(1)} collective-permute-done((bf16[128,1024]{1,0:T(8,128)(2,1)S(1)}, bf16[128,1024]{1,0:T(8,128)(2,1)S(1)}, u32[]{:S(2)}, u32[]{:S(2)}) %collective-permute-start.3) | collective-permute-done | bytes 262176 | tf_op jit(solution)/shard_map/ppermute | solution.py:14
  213.8 1.0 maximum_bitcast_fusion
  (2 shorter events, 0.0 us)
Async XLA Ops:
  6.5 81.1 %all-gather.3.cloned.1.call-start = ((), (), s32[]{:S(2)}) async-start(), calls=%async_computation | async-start | bytes 2396160 | tf_op jit(solution)/shard_map/all_gather | solution.py:77
  106.2 14.2 %copy-start.2 = (bf16[128,1024]{1,0:T(8,128)(2,1)S(1)}, bf16[128,1024]{1,0:T(8,128)(2,1)}, u32[]{:S(2)}) copy-start(bf16[128,1024]{1,0:T(8,128)(2,1)} %shard_map.47) | copy-start | bytes 786436
  106.2 20.3 %copy-start.1 = (bf16[128,1024]{1,0:T(8,128)(2,1)S(1)}, bf16[128,1024]{1,0:T(8,128)(2,1)}, u32[]{:S(2)}) copy-start(bf16[128,1024]{1,0:T(8,128)(2,1)} %shard_map.48) | copy-start | bytes 786436
  106.2 29.2 %copy-start = (bf16[128,1024]{1,0:T(8,128)(2,1)S(1)}, bf16[128,1024]{1,0:T(8,128)(2,1)}, u32[]{:S(2)}) copy-start(bf16[128,1024]{1,0:T(8,128)(2,1)} %shard_map.49) | copy-start | bytes 786436
  111.7 76.6 %collective-permute-start = (bf16[128,1024]{1,0:T(8,128)(2,1)}, bf16[128,1024]{1,0:T(8,128)(2,1)S(1)}, u32[]{:S(2)}, u32[]{:S(2)}) collective-permute-start(bf16[128,1024]{1,0:T(8,128)(2,1)} %shard_map.46), channel_id=1, source_target_pairs={{960,0},{0,64},{64,128},{128,192},{192,256},{256,320},{320,384},{3... | collective-permute-start | bytes 786440 | tf_op jit(solution)/shard_map/ppermute | solution.py:14
  120.4 82.1 %collective-permute-start.1 = (bf16[128,1024]{1,0:T(8,128)(2,1)S(1)}, bf16[128,1024]{1,0:T(8,128)(2,1)S(1)}, u32[]{:S(2)}, u32[]{:S(2)}) collective-permute-start(bf16[128,1024]{1,0:T(8,128)(2,1)S(1)} %copy-done.2), channel_id=1, source_target_pairs={{960,0},{0,64},{64,128},{128,192},{192,256},{256,320},{320,384},{3... | collective-permute-start | bytes 786440 | tf_op jit(solution)/shard_map/ppermute | solution.py:14
  126.5 81.7 %collective-permute-start.2 = (bf16[128,1024]{1,0:T(8,128)(2,1)S(1)}, bf16[128,1024]{1,0:T(8,128)(2,1)S(1)}, u32[]{:S(2)}, u32[]{:S(2)}) collective-permute-start(bf16[128,1024]{1,0:T(8,128)(2,1)S(1)} %copy-done.1), channel_id=1, source_target_pairs={{960,0},{0,64},{64,128},{128,192},{192,256},{256,320},{320,384},{3... | collective-permute-start | bytes 786440 | tf_op jit(solution)/shard_map/ppermute | solution.py:14
  135.4 78.4 %collective-permute-start.3 = (bf16[128,1024]{1,0:T(8,128)(2,1)S(1)}, bf16[128,1024]{1,0:T(8,128)(2,1)S(1)}, u32[]{:S(2)}, u32[]{:S(2)}) collective-permute-start(bf16[128,1024]{1,0:T(8,128)(2,1)S(1)} %copy-done), channel_id=1, source_target_pairs={{960,0},{0,64},{64,128},{128,192},{192,256},{256,320},{320,384},{3... | collective-permute-start | bytes 786440 | tf_op jit(solution)/shard_map/ppermute | solution.py:14
Sparse Core Ops, SparseCore 0:
  10.0 77.5 all-gather.2

commit v5 on v4

--- a/solution.py
+++ b/solution.py
@@ -19,12 +19,11 @@
     return jnp.sum(jnp.where(segments[:, None] == levels[None, :], limits[None, :], 0), axis=1)
 
 
-def attention_kernel(q_ref, g_ref, b_ref, o_ref, *, head, groups, head_size, scale):
+def attention_kernel(q_ref, g_ref, b_ref, o_ref, *, groups, head_size, scale):
     parts = g_ref.shape[0]
     span = parts * head_size
-    k_at = head * 2 * head_size
-    k = g_ref[:, k_at : k_at + head_size, :].reshape(span, head_size)
-    v = g_ref[:, k_at + head_size : k_at + 2 * head_size, :].reshape(span, head_size)
+    k = g_ref[:, :head_size, :].reshape(span, head_size)
+    v = g_ref[:, head_size:, :].reshape(span, head_size)
     bias = b_ref[...]
     for g in range(groups):
         qg = q_ref[:, g * head_size : (g + 1) * head_size]
@@ -37,19 +36,19 @@
         o_ref[:, g * head_size : (g + 1) * head_size] = (pv / total).astype(o_ref.dtype)
 
 
-def attention_head(q, gathered, bias, head, kv_heads, head_size):
+def attention_head(q, gathered, bias, head, local, kv_heads, head_size):
     rows, width = q.shape
     groups = width // head_size // kv_heads
     block = groups * head_size
     kernel = functools.partial(
-        attention_kernel, head=head, groups=groups, head_size=head_size, scale=1.0 / math.sqrt(head_size)
+        attention_kernel, groups=groups, head_size=head_size, scale=1.0 / math.sqrt(head_size)
     )
     return pl.pallas_call(
         kernel,
         grid=(1,),
         in_specs=[
             pl.BlockSpec((rows, block), lambda i: (0, head)),
-            pl.BlockSpec(gathered.shape, lambda i: (0, 0, 0)),
+            pl.BlockSpec((gathered.shape[0], 2 * head_size, gathered.shape[2]), lambda i: (0, local, 0)),
             pl.BlockSpec(bias.shape, lambda i: (0, 0)),
         ],
         out_specs=pl.BlockSpec((rows, block), lambda i: (0, 0)),
@@ -70,12 +69,13 @@
     tensor_size = lax.axis_size("tensor")
 
     body = pairs.reshape(rows, kv_heads, 2, head_size).transpose(1, 2, 0, 3).reshape(-1, head_size)
+    half = kv_heads // 2
+    half_rows = half * 2 * rows
     extra = jnp.zeros((16, lane), jnp.bfloat16)
     extra = extra.at[0, :rows].set(segments.astype(jnp.bfloat16))
-    packed = jnp.concatenate([body, extra], axis=0)
-    body_rows = body.shape[0]
-    gathered = lax.all_gather(packed, "tensor", axis=0, tiled=False)
-    key_segment = gathered[:, body_rows, :rows].reshape(tensor_size * rows).astype(jnp.int32)
+    first = lax.all_gather(jnp.concatenate([body[:half_rows], extra], axis=0), "tensor", axis=0, tiled=False)
+    second = lax.all_gather(body[half_rows:], "tensor", axis=0, tiled=False)
+    key_segment = first[:, half_rows, :rows].reshape(tensor_size * rows).astype(jnp.int32)
 
     my_first = lax.axis_index("tensor") * rows
     query_pos = my_first + jnp.arange(rows)
@@ -88,7 +88,8 @@
 
     pieces = []
     for h in range(kv_heads):
-        out_h = attention_head(query_rows, gathered, mask_bias, h, kv_heads, head_size)
+        source = first if h < half else second
+        out_h = attention_head(query_rows, source, mask_bias, h, h % half, kv_heads, head_size)
         pieces.append(from_behind(out_h, "section", 1))
     return jnp.concatenate(pieces, axis=1)[None]
 

time: 222 us -> 244 us (1.099)
  waiting for transfers between devices: 150 us -> 175 us
    all_gather x1 -> x2, waiting for transfers between devices: 77.8 us -> 139 us  [the longest x1 73 us: attend(): lax.all_gather(jnp.concatenate([body[:half_rows], extra], axis=0), 'tenso...]
    ppermute x4, waiting for transfers between devices: 72.4 us -> 36 us  [from_behind(): return lax.ppermute(block, axis, route)]
  transfers between devices with their start and end apart: 5 -> 6, of which waited for: 5 -> 4; matrix products, arithmetic and copies ran while one was open for 0% -> 1% of each run, Pallas kernels for 0% -> 8%
where the time goes in v5:
time: 244 us
  waiting for transfers between devices  175 us (72%)
  starting transfers between devices  29.7 us (12%)
  Pallas kernels  19.7 us (8%)
  between operations  13.5 us (6%)
  other arithmetic  3.53 us (1%)
    all_gather x1, waiting for transfers between devices, attend(): lax.all_gather(jnp.concatenate([body[:half_rows], extra], axis=0), 'tenso...  73 us
    all_gather x1, waiting for transfers between devices, attend(): second = lax.all_gather(body[half_rows:], 'tensor', axis=0, tiled=False)  65.6 us
    ppermute x4, waiting for transfers between devices, from_behind(): return lax.ppermute(block, axis, route)  36 us
    ppermute x4, starting transfers between devices, from_behind(): return lax.ppermute(block, axis, route)  29.6 us
    pallas_call x4, Pallas kernels, attention_head(): pl.pallas_call(kernel, grid=(1,), in_specs=[pl.BlockSpec((rows, block), l...  19.7 us
  transfers between devices with their start and end apart: 6, of which 4 were waited for; matrix products, arithmetic and copies ran while one was open for 1% of the time, Pallas kernels for 8%

profile of v5, /device:TPU:1, one launch (start us, length us, event | category | flops | bytes accessed | tf_op | source)
XLA Modules:
  0.0 243.5 jit_solution(15705139582468969629)
XLA Ops:
  6.5 0.0 copy-start.1
  6.5 0.0 copy-start.2
  6.5 0.0 all-gather.6.cloned.1.call-start
  6.5 1.1 reshape_squeeze.4
  7.7 0.7 fusion.5
  8.3 0.0 copy-done.1
  8.3 0.7 fusion.4
  9.0 0.0 all-gather.6.cloned.1.call-update
  9.0 0.0 all-gather.4.cloned.1.call-start
  9.1 0.7 all-gather.4.cloned.1.call-update
  9.8 0.0 copy-done.2
  9.8 0.1 select_reduce_fusion
  9.9 73.0 %all-gather.6.cloned.1.call-done = bf16[4224,128]{1,0:T(8,128)(2,1)} async-done(((bf16[528,128]{1,0:T(8,128)(2,1)}), bf16[4224,128]{1,0:T(8,128)(2,1)}) %all-gather.6.cloned.1.call-update) | async-done | bytes 1081360 | tf_op jit(solution)/shard_map/all_gather | solution.py:76
  82.9 0.7 slice_convert_fusion
  83.7 1.0 fusion.2.b_ref
  84.7 4.9 %shard_map.46 = bf16[128,1024]{1,0:T(8,128)(2,1)} custom-call(bf16[128,4096]{1,0:T(8,128)(2,1)} %bitcast.12, bf16[8,528,128]{2,1,0:T(8,128)(2,1)} %bitcast.17, f32[128,1024]{1,0:T(8,128)} %fusion.2.b_ref), custom_call_target="tpu_custom_call" | custom-call | tf_op jit(solution)/shard_map/pallas_call | solution.py:46
  89.6 0.0 copy-start
  89.6 5.0 %shard_map.47 = bf16[128,1024]{1,0:T(8,128)(2,1)} custom-call(bf16[128,4096]{1,0:T(8,128)(2,1)} %bitcast.13, bf16[8,528,128]{2,1,0:T(8,128)(2,1)} %bitcast.18, f32[128,1024]{1,0:T(8,128)} %fusion.2.b_ref), custom_call_target="tpu_custom_call" | custom-call | tf_op jit(solution)/shard_map/pallas_call | solution.py:46
  94.5 0.0 copy-done
  94.5 7.0 %collective-permute-start = (bf16[128,1024]{1,0:T(8,128)(2,1)S(1)}, bf16[128,1024]{1,0:T(8,128)(2,1)S(1)}, u32[]{:S(2)}, u32[]{:S(2)}) collective-permute-start(bf16[128,1024]{1,0:T(8,128)(2,1)S(1)} %copy-done), channel_id=1, source_target_pairs={{960,0},{0,64},{64,128},{128,192},{192,256},{256,320},{320,384},{3... | collective-permute-start | bytes 786440 | tf_op jit(solution)/shard_map/ppermute | solution.py:14
  101.5 7.8 %collective-permute-start.1 = (bf16[128,1024]{1,0:T(8,128)(2,1)}, bf16[128,1024]{1,0:T(8,128)(2,1)S(1)}, u32[]{:S(2)}, u32[]{:S(2)}) collective-permute-start(bf16[128,1024]{1,0:T(8,128)(2,1)} %shard_map.47), channel_id=1, source_target_pairs={{960,0},{0,64},{64,128},{128,192},{192,256},{256,320},{320,384},{3... | collective-permute-start | bytes 786440 | tf_op jit(solution)/shard_map/ppermute | solution.py:14
  109.3 65.6 %all-gather.4.cloned.1.call-done.g_ref = bf16[8,512,128]{2,1,0:T(8,128)(2,1)} async-done(((bf16[1,512,128]{2,1,0:T(8,128)(2,1)}), bf16[8,512,128]{2,1,0:T(8,128)(2,1)}) %all-gather.4.cloned.1.call-update) | async-done | bytes 1048592 | tf_op jit(solution)/shard_map/all_gather | solution.py:77
  174.9 4.9 %shard_map.48 = bf16[128,1024]{1,0:T(8,128)(2,1)} custom-call(bf16[128,4096]{1,0:T(8,128)(2,1)} %bitcast.14, bf16[8,512,128]{2,1,0:T(8,128)(2,1)} %all-gather.4.cloned.1.call-done.g_ref, f32[128,1024]{1,0:T(8,128)} %fusion.2.b_ref), custom_call_target="tpu_custom_call" | custom-call | tf_op jit(solution)/shard_map/pallas_call | solution.py:46
  179.8 7.9 %collective-permute-start.2 = (bf16[128,1024]{1,0:T(8,128)(2,1)}, bf16[128,1024]{1,0:T(8,128)(2,1)S(1)}, u32[]{:S(2)}, u32[]{:S(2)}) collective-permute-start(bf16[128,1024]{1,0:T(8,128)(2,1)} %shard_map.48), channel_id=1, source_target_pairs={{960,0},{0,64},{64,128},{128,192},{192,256},{256,320},{320,384},{3... | collective-permute-start | bytes 786440 | tf_op jit(solution)/shard_map/ppermute | solution.py:14
  187.7 4.9 %shard_map.49 = bf16[128,1024]{1,0:T(8,128)(2,1)} custom-call(bf16[128,4096]{1,0:T(8,128)(2,1)} %bitcast.15, bf16[8,512,128]{2,1,0:T(8,128)(2,1)} %all-gather.4.cloned.1.call-done.g_ref, f32[128,1024]{1,0:T(8,128)} %fusion.2.b_ref), custom_call_target="tpu_custom_call" | custom-call | tf_op jit(solution)/shard_map/pallas_call | solution.py:46
  192.7 7.0 %collective-permute-start.3 = (bf16[128,1024]{1,0:T(8,128)(2,1)}, bf16[128,1024]{1,0:T(8,128)(2,1)S(1)}, u32[]{:S(2)}, u32[]{:S(2)}) collective-permute-start(bf16[128,1024]{1,0:T(8,128)(2,1)} %shard_map.49), channel_id=1, source_target_pairs={{960,0},{0,64},{64,128},{128,192},{192,256},{256,320},{320,384},{3... | collective-permute-start | bytes 786440 | tf_op jit(solution)/shard_map/ppermute | solution.py:14
  199.7 0.0 collective-permute-done
  199.7 0.0 collective-permute-done.1
  199.7 28.8 %collective-permute-done.2 = bf16[128,1024]{1,0:T(8,128)(2,1)S(1)} collective-permute-done((bf16[128,1024]{1,0:T(8,128)(2,1)}, bf16[128,1024]{1,0:T(8,128)(2,1)S(1)}, u32[]{:S(2)}, u32[]{:S(2)}) %collective-permute-start.2) | collective-permute-done | bytes 262176 | tf_op jit(solution)/shard_map/ppermute | solution.py:14
  228.4 7.2 %collective-permute-done.3 = bf16[128,1024]{1,0:T(8,128)(2,1)S(1)} collective-permute-done((bf16[128,1024]{1,0:T(8,128)(2,1)}, bf16[128,1024]{1,0:T(8,128)(2,1)S(1)}, u32[]{:S(2)}, u32[]{:S(2)}) %collective-permute-start.3) | collective-permute-done | bytes 262176 | tf_op jit(solution)/shard_map/ppermute | solution.py:14
  235.7 1.0 maximum_bitcast_fusion
  (3 shorter events, 0.0 us)
Async XLA Ops:
  6.5 1.8 copy-start.1
  6.5 3.3 %copy-start.2 = (s32[1,4]{1,0:T(1,128)S(1)}, s32[1,4]{1,0:T(1,128)}, u32[]{:S(2)}) copy-start(s32[1,4]{1,0:T(1,128)} %param.9) | copy-start | bytes 52
  6.5 76.4 %all-gather.6.cloned.1.call-start = ((), (), s32[]{:S(2)}) async-start(), calls=%async_computation.1 | async-start | bytes 1216512 | tf_op jit(solution)/shard_map/all_gather | solution.py:76
  9.0 165.9 %all-gather.4.cloned.1.call-start = ((), (), s32[]{:S(2)}) async-start(), calls=%async_computation | async-start | bytes 1179648 | tf_op jit(solution)/shard_map/all_gather | solution.py:77
  89.6 5.0 %copy-start = (bf16[128,1024]{1,0:T(8,128)(2,1)S(1)}, bf16[128,1024]{1,0:T(8,128)(2,1)}, u32[]{:S(2)}) copy-start(bf16[128,1024]{1,0:T(8,128)(2,1)} %shard_map.46) | copy-start | bytes 786436
  94.5 105.1 %collective-permute-start = (bf16[128,1024]{1,0:T(8,128)(2,1)S(1)}, bf16[128,1024]{1,0:T(8,128)(2,1)S(1)}, u32[]{:S(2)}, u32[]{:S(2)}) collective-permute-start(bf16[128,1024]{1,0:T(8,128)(2,1)S(1)} %copy-done), channel_id=1, source_target_pairs={{960,0},{0,64},{64,128},{128,192},{192,256},{256,320},{320,384},{3... | collective-permute-start | bytes 786440 | tf_op jit(solution)/shard_map/ppermute | solution.py:14
  101.5 98.1 %collective-permute-start.1 = (bf16[128,1024]{1,0:T(8,128)(2,1)}, bf16[128,1024]{1,0:T(8,128)(2,1)S(1)}, u32[]{:S(2)}, u32[]{:S(2)}) collective-permute-start(bf16[128,1024]{1,0:T(8,128)(2,1)} %shard_map.47), channel_id=1, source_target_pairs={{960,0},{0,64},{64,128},{128,192},{192,256},{256,320},{320,384},{3... | collective-permute-start | bytes 786440 | tf_op jit(solution)/shard_map/ppermute | solution.py:14
  179.8 48.6 %collective-permute-start.2 = (bf16[128,1024]{1,0:T(8,128)(2,1)}, bf16[128,1024]{1,0:T(8,128)(2,1)S(1)}, u32[]{:S(2)}, u32[]{:S(2)}) collective-permute-start(bf16[128,1024]{1,0:T(8,128)(2,1)} %shard_map.48), channel_id=1, source_target_pairs={{960,0},{0,64},{64,128},{128,192},{192,256},{256,320},{320,384},{3... | collective-permute-start | bytes 786440 | tf_op jit(solution)/shard_map/ppermute | solution.py:14
  192.7 43.0 %collective-permute-start.3 = (bf16[128,1024]{1,0:T(8,128)(2,1)}, bf16[128,1024]{1,0:T(8,128)(2,1)S(1)}, u32[]{:S(2)}, u32[]{:S(2)}) collective-permute-start(bf16[128,1024]{1,0:T(8,128)(2,1)} %shard_map.49), channel_id=1, source_target_pairs={{960,0},{0,64},{64,128},{128,192},{192,256},{256,320},{320,384},{3... | collective-permute-start | bytes 786440 | tf_op jit(solution)/shard_map/ppermute | solution.py:14
Sparse Core Ops, SparseCore 0:
  10.0 72.8 all-gather.5
  85.6 89.2 all-gather.3

commit v6 on v4

v6 whole, which is shorter than its diff:
```python
import functools
import math

import jax
import jax.numpy as jnp
from jax import lax
from jax.experimental import pallas as pl
from jax.sharding import PartitionSpec as P


def from_behind(block, axis, distance):
    devices = range(lax.axis_size(axis))
    route = [((i - distance) % len(devices), i) for i in devices]
    return lax.ppermute(block, axis, route)


def bound_of(segments, limits):
    levels = jnp.arange(limits.shape[0])
    return jnp.sum(jnp.where(segments[:, None] == levels[None, :], limits[None, :], 0), axis=1)


def attention_kernel(q_ref, g_ref, s_ref, i_ref, o_ref, *, groups, head_size, scale):
    parts = g_ref.shape[0]
    span = parts * head_size
    k = g_ref[:, :head_size, :].reshape(span, head_size)
    v = g_ref[:, head_size:, :].reshape(span, head_size)
    own = i_ref[:, 0:1]
    place = i_ref[:, 1:2]
    reach = i_ref[:, 2:3]
    blocks = []
    for p in range(parts):
        key_seg = s_ref[p, 0:1, :].astype(jnp.int32)
        key_pos = p * head_size + lax.broadcasted_iota(jnp.int32, (1, head_size), 1)
        seen = (own == key_seg) & ((key_pos <= place) | (key_pos <= reach))
        blocks.append(jnp.where(seen, 0.0, -1e30).astype(jnp.float32))
    bias = jnp.concatenate(blocks, axis=1)
    for g in range(groups):
        qg = q_ref[:, g * head_size : (g + 1) * head_size]
        s = lax.dot_general(qg, k, (((1,), (1,)), ((), ())), preferred_element_type=jnp.float32)
        s = s * scale + bias
        m = jnp.max(s, axis=1, keepdims=True)
        w = jnp.exp(s - m)
        total = jnp.sum(w, axis=1, keepdims=True)
        pv = jnp.dot(w.astype(jnp.bfloat16), v, preferred_element_type=jnp.float32)
        o_ref[:, g * head_size : (g + 1) * head_size] = (pv / total).astype(o_ref.dtype)


def attention_head(q, gathered, info, head, id_row, kv_heads, head_size):
    rows, width = q.shape
    groups = width // head_size // kv_heads
    block = groups * head_size
    kernel = functools.partial(
        attention_kernel, groups=groups, head_size=head_size, scale=1.0 / math.sqrt(head_size)
    )
    return pl.pallas_call(
        kernel,
        grid=(1,),
        in_specs=[
            pl.BlockSpec((rows, block), lambda i: (0, head)),
            pl.BlockSpec((gathered.shape[0], 2 * head_size, gathered.shape[2]), lambda i: (0, head, 0)),
            pl.BlockSpec((gathered.shape[0], 16, gathered.shape[2]), lambda i: (0, id_row // 16, 0)),
            pl.BlockSpec(info.shape, lambda i: (0, 0)),
        ],
        out_specs=pl.BlockSpec((rows, block), lambda i: (0, 0)),
        out_shape=jax.ShapeDtypeStruct((rows, block), jnp.bfloat16),
    )(q, gathered, gathered, info)


def attend(queries, keys_values, segment_ids, bounds):
    query_rows = queries[0]
    pairs = keys_values[0]
    segments = segment_ids[0]
    limits = bounds[0]
    rows = query_rows.shape[0]
    kv_heads = pairs.shape[1]
    width = pairs.shape[2]
    head_size = width // 2
    lane = 128

    body = pairs.reshape(rows, kv_heads, 2, head_size).transpose(1, 2, 0, 3).reshape(-1, head_size)
    extra = jnp.zeros((16, lane), jnp.bfloat16)
    extra = extra.at[0, :rows].set(segments.astype(jnp.bfloat16))
    packed = jnp.concatenate([body, extra], axis=0)
    body_rows = body.shape[0]
    gathered = lax.all_gather(packed, "tensor", axis=0, tiled=False)

    my_first = lax.axis_index("tensor") * rows
    query_pos = my_first + jnp.arange(rows)
    query_bound = bound_of(segments, limits)
    info = jnp.stack([segments, query_pos, query_bound], axis=1).astype(jnp.int32)

    pieces = []
    for h in range(kv_heads):
        out_h = attention_head(query_rows, gathered, info, h, body_rows, kv_heads, head_size)
        pieces.append(from_behind(out_h, "section", 1))
    return jnp.concatenate(pieces, axis=1)[None]


def solution(mesh):
    in_specs = (
        P("section", ("dp", "tensor"), None),
        P("section", ("dp", "tensor"), None, None),
        P("section", ("dp", "tensor")),
        P("section", "dp"),
    )
    out_specs = P("section", ("dp", "tensor"), None)
    return jax.shard_map(attend, mesh=mesh, in_specs=in_specs, out_specs=out_specs, check_vma=False)
```

time: 222 us -> 217 us (0.977)
  Pallas kernels: 21.7 us -> 19.4 us
    pallas_call x4, Pallas kernels: 21.7 us -> 19.4 us  [attention_head(): pl.pallas_call(kernel, grid=(1,), in_specs=[pl.BlockSpec((rows, block), l...]
  transfers between devices with their start and end apart: 5 -> 5, of which waited for: 5 -> 5; matrix products, arithmetic and copies ran while one was open for 0% -> 1% of each run, Pallas kernels for 0% -> 0%
where the time goes in v6:
time: 217 us
  waiting for transfers between devices  149 us (69%)
  starting transfers between devices  29.7 us (14%)
  Pallas kernels  19.4 us (9%)
  between operations  13.5 us (6%)
  other arithmetic  3.85 us (2%)
    all_gather x1, waiting for transfers between devices, attend(): gathered = lax.all_gather(packed, 'tensor', axis=0, tiled=False)  76.4 us
    ppermute x4, waiting for transfers between devices, from_behind(): return lax.ppermute(block, axis, route)  72.4 us
    ppermute x4, starting transfers between devices, from_behind(): return lax.ppermute(block, axis, route)  29.7 us
    pallas_call x4, Pallas kernels, attention_head(): pl.pallas_call(kernel, grid=(1,), in_specs=[pl.BlockSpec((rows, block), l...  19.4 us
  transfers between devices with their start and end apart: 5, of which 5 were waited for; matrix products, arithmetic and copies ran while one was open for 1% of the time, Pallas kernels for 0%

profile of v6, /device:TPU:1, one launch (start us, length us, event | category | flops | bytes accessed | tf_op | source)
XLA Modules:
  0.0 217.0 jit_solution(2279383303135907211)
XLA Ops:
  6.5 0.0 all-gather.3.cloned.1.call-start
  6.5 0.7 convert_element_type.4
  7.2 1.1 reshape_squeeze.3
  8.3 0.7 fusion.1
  9.0 0.0 all-gather.3.cloned.1.call-update
  9.1 0.8 select_reduce_fusion
  9.8 0.7 pad_add_fusion
  10.5 0.7 copy.14.i_ref
  11.2 76.4 %all-gather.3.cloned.1.call-done = bf16[8320,128]{1,0:T(8,128)(2,1)} async-done(((bf16[1040,128]{1,0:T(8,128)(2,1)}), bf16[8320,128]{1,0:T(8,128)(2,1)}) %all-gather.3.cloned.1.call-update) | async-done | bytes 2129936 | tf_op jit(solution)/shard_map/all_gather | solution.py:85
  87.6 4.8 %shard_map.49 = bf16[128,1024]{1,0:T(8,128)(2,1)} custom-call(bf16[128,4096]{1,0:T(8,128)(2,1)} %bitcast.18, bf16[8,1040,128]{2,1,0:T(8,128)(2,1)} %bitcast.10, bf16[8,1040,128]{2,1,0:T(8,128)(2,1)} %bitcast.11, s32[128,3]{1,0:T(8,128)} %copy.14.i_ref), custom_call_target="tpu_custom_call" | custom-call | tf_op jit(solution)/shard_map/pallas_call | solution.py:55
  92.4 4.8 %shard_map.48 = bf16[128,1024]{1,0:T(8,128)(2,1)} custom-call(bf16[128,4096]{1,0:T(8,128)(2,1)} %bitcast.19, bf16[8,1040,128]{2,1,0:T(8,128)(2,1)} %bitcast.12, bf16[8,1040,128]{2,1,0:T(8,128)(2,1)} %bitcast.13, s32[128,3]{1,0:T(8,128)} %copy.14.i_ref), custom_call_target="tpu_custom_call" | custom-call | tf_op jit(solution)/shard_map/pallas_call | solution.py:55
  97.3 4.8 %shard_map.47 = bf16[128,1024]{1,0:T(8,128)(2,1)} custom-call(bf16[128,4096]{1,0:T(8,128)(2,1)} %bitcast.20, bf16[8,1040,128]{2,1,0:T(8,128)(2,1)} %bitcast.14, bf16[8,1040,128]{2,1,0:T(8,128)(2,1)} %bitcast.15, s32[128,3]{1,0:T(8,128)} %copy.14.i_ref), custom_call_target="tpu_custom_call" | custom-call | tf_op jit(solution)/shard_map/pallas_call | solution.py:55
  102.1 0.0 copy-start.2
  102.1 0.0 copy-start.1
  102.1 0.0 copy-start
  102.1 4.9 %shard_map.46 = bf16[128,1024]{1,0:T(8,128)(2,1)} custom-call(bf16[128,4096]{1,0:T(8,128)(2,1)} %bitcast.21, bf16[8,1040,128]{2,1,0:T(8,128)(2,1)} %bitcast.16, bf16[8,1040,128]{2,1,0:T(8,128)(2,1)} %bitcast.17, s32[128,3]{1,0:T(8,128)} %copy.14.i_ref), custom_call_target="tpu_custom_call" | custom-call | tf_op jit(solution)/shard_map/pallas_call | solution.py:55
  107.0 8.7 %collective-permute-start = (bf16[128,1024]{1,0:T(8,128)(2,1)}, bf16[128,1024]{1,0:T(8,128)(2,1)S(1)}, u32[]{:S(2)}, u32[]{:S(2)}) collective-permute-start(bf16[128,1024]{1,0:T(8,128)(2,1)} %shard_map.46), channel_id=1, source_target_pairs={{960,0},{0,64},{64,128},{128,192},{192,256},{256,320},{320,384},{3... | collective-permute-start | bytes 786440 | tf_op jit(solution)/shard_map/ppermute | solution.py:14
  115.7 0.0 copy-done.2
  115.7 6.1 %collective-permute-start.1 = (bf16[128,1024]{1,0:T(8,128)(2,1)S(1)}, bf16[128,1024]{1,0:T(8,128)(2,1)S(1)}, u32[]{:S(2)}, u32[]{:S(2)}) collective-permute-start(bf16[128,1024]{1,0:T(8,128)(2,1)S(1)} %copy-done.2), channel_id=1, source_target_pairs={{960,0},{0,64},{64,128},{128,192},{192,256},{256,320},{320,384},{3... | collective-permute-start | bytes 786440 | tf_op jit(solution)/shard_map/ppermute | solution.py:14
  121.8 0.0 copy-done.1
  121.8 8.9 %collective-permute-start.2 = (bf16[128,1024]{1,0:T(8,128)(2,1)S(1)}, bf16[128,1024]{1,0:T(8,128)(2,1)S(1)}, u32[]{:S(2)}, u32[]{:S(2)}) collective-permute-start(bf16[128,1024]{1,0:T(8,128)(2,1)S(1)} %copy-done.1), channel_id=1, source_target_pairs={{960,0},{0,64},{64,128},{128,192},{192,256},{256,320},{320,384},{3... | collective-permute-start | bytes 786440 | tf_op jit(solution)/shard_map/ppermute | solution.py:14
  130.7 0.0 copy-done
  130.7 6.1 %collective-permute-start.3 = (bf16[128,1024]{1,0:T(8,128)(2,1)S(1)}, bf16[128,1024]{1,0:T(8,128)(2,1)S(1)}, u32[]{:S(2)}, u32[]{:S(2)}) collective-permute-start(bf16[128,1024]{1,0:T(8,128)(2,1)S(1)} %copy-done), channel_id=1, source_target_pairs={{960,0},{0,64},{64,128},{128,192},{192,256},{256,320},{320,384},{3... | collective-permute-start | bytes 786440 | tf_op jit(solution)/shard_map/ppermute | solution.py:14
  136.7 46.9 %collective-permute-done = bf16[128,1024]{1,0:T(8,128)(2,1)S(1)} collective-permute-done((bf16[128,1024]{1,0:T(8,128)(2,1)}, bf16[128,1024]{1,0:T(8,128)(2,1)S(1)}, u32[]{:S(2)}, u32[]{:S(2)}) %collective-permute-start) | collective-permute-done | bytes 262176 | tf_op jit(solution)/shard_map/ppermute | solution.py:14
  183.6 14.3 %collective-permute-done.1 = bf16[128,1024]{1,0:T(8,128)(2,1)S(1)} collective-permute-done((bf16[128,1024]{1,0:T(8,128)(2,1)S(1)}, bf16[128,1024]{1,0:T(8,128)(2,1)S(1)}, u32[]{:S(2)}, u32[]{:S(2)}) %collective-permute-start.1) | collective-permute-done | bytes 262176 | tf_op jit(solution)/shard_map/ppermute | solution.py:14
  197.9 5.6 %collective-permute-done.2 = bf16[128,1024]{1,0:T(8,128)(2,1)S(1)} collective-permute-done((bf16[128,1024]{1,0:T(8,128)(2,1)S(1)}, bf16[128,1024]{1,0:T(8,128)(2,1)S(1)}, u32[]{:S(2)}, u32[]{:S(2)}) %collective-permute-start.2) | collective-permute-done | bytes 262176 | tf_op jit(solution)/shard_map/ppermute | solution.py:14
  203.5 5.6 %collective-permute-done.3 = bf16[128,1024]{1,0:T(8,128)(2,1)S(1)} collective-permute-done((bf16[128,1024]{1,0:T(8,128)(2,1)S(1)}, bf16[128,1024]{1,0:T(8,128)(2,1)S(1)}, u32[]{:S(2)}, u32[]{:S(2)}) %collective-permute-start.3) | collective-permute-done | bytes 262176 | tf_op jit(solution)/shard_map/ppermute | solution.py:14
  209.1 1.0 maximum_bitcast_fusion
  (2 shorter events, 0.0 us)
Async XLA Ops:
  6.5 81.1 %all-gather.3.cloned.1.call-start = ((), (), s32[]{:S(2)}) async-start(), calls=%async_computation | async-start | bytes 2396160 | tf_op jit(solution)/shard_map/all_gather | solution.py:85
  102.1 13.6 %copy-start.2 = (bf16[128,1024]{1,0:T(8,128)(2,1)S(1)}, bf16[128,1024]{1,0:T(8,128)(2,1)}, u32[]{:S(2)}) copy-start(bf16[128,1024]{1,0:T(8,128)(2,1)} %shard_map.47) | copy-start | bytes 786436
  102.1 19.7 %copy-start.1 = (bf16[128,1024]{1,0:T(8,128)(2,1)S(1)}, bf16[128,1024]{1,0:T(8,128)(2,1)}, u32[]{:S(2)}) copy-start(bf16[128,1024]{1,0:T(8,128)(2,1)} %shard_map.48) | copy-start | bytes 786436
  102.1 28.6 %copy-start = (bf16[128,1024]{1,0:T(8,128)(2,1)S(1)}, bf16[128,1024]{1,0:T(8,128)(2,1)}, u32[]{:S(2)}) copy-start(bf16[128,1024]{1,0:T(8,128)(2,1)} %shard_map.49) | copy-start | bytes 786436
  107.0 76.6 %collective-permute-start = (bf16[128,1024]{1,0:T(8,128)(2,1)}, bf16[128,1024]{1,0:T(8,128)(2,1)S(1)}, u32[]{:S(2)}, u32[]{:S(2)}) collective-permute-start(bf16[128,1024]{1,0:T(8,128)(2,1)} %shard_map.46), channel_id=1, source_target_pairs={{960,0},{0,64},{64,128},{128,192},{192,256},{256,320},{320,384},{3... | collective-permute-start | bytes 786440 | tf_op jit(solution)/shard_map/ppermute | solution.py:14
  115.7 82.1 %collective-permute-start.1 = (bf16[128,1024]{1,0:T(8,128)(2,1)S(1)}, bf16[128,1024]{1,0:T(8,128)(2,1)S(1)}, u32[]{:S(2)}, u32[]{:S(2)}) collective-permute-start(bf16[128,1024]{1,0:T(8,128)(2,1)S(1)} %copy-done.2), channel_id=1, source_target_pairs={{960,0},{0,64},{64,128},{128,192},{192,256},{256,320},{320,384},{3... | collective-permute-start | bytes 786440 | tf_op jit(solution)/shard_map/ppermute | solution.py:14
  121.8 81.7 %collective-permute-start.2 = (bf16[128,1024]{1,0:T(8,128)(2,1)S(1)}, bf16[128,1024]{1,0:T(8,128)(2,1)S(1)}, u32[]{:S(2)}, u32[]{:S(2)}) collective-permute-start(bf16[128,1024]{1,0:T(8,128)(2,1)S(1)} %copy-done.1), channel_id=1, source_target_pairs={{960,0},{0,64},{64,128},{128,192},{192,256},{256,320},{320,384},{3... | collective-permute-start | bytes 786440 | tf_op jit(solution)/shard_map/ppermute | solution.py:14
  130.7 78.4 %collective-permute-start.3 = (bf16[128,1024]{1,0:T(8,128)(2,1)S(1)}, bf16[128,1024]{1,0:T(8,128)(2,1)S(1)}, u32[]{:S(2)}, u32[]{:S(2)}) collective-permute-start(bf16[128,1024]{1,0:T(8,128)(2,1)S(1)} %copy-done), channel_id=1, source_target_pairs={{960,0},{0,64},{64,128},{128,192},{192,256},{256,320},{320,384},{3... | collective-permute-start | bytes 786440 | tf_op jit(solution)/shard_map/ppermute | solution.py:14
Sparse Core Ops, SparseCore 0:
  10.0 77.5 all-gather.2

commit v7 on v6

--- a/solution.py
+++ b/solution.py
@@ -45,10 +45,11 @@
         o_ref[:, g * head_size : (g + 1) * head_size] = (pv / total).astype(o_ref.dtype)
 
 
-def attention_head(q, gathered, info, head, id_row, kv_heads, head_size):
+def attention_head(q, gathered, info, first, count, id_row, kv_heads, head_size):
     rows, width = q.shape
-    groups = width // head_size // kv_heads
+    groups = count
     block = groups * head_size
+    head = first // (width // head_size // kv_heads)
     kernel = functools.partial(
         attention_kernel, groups=groups, head_size=head_size, scale=1.0 / math.sqrt(head_size)
     )
@@ -56,7 +57,7 @@
         kernel,
         grid=(1,),
         in_specs=[
-            pl.BlockSpec((rows, block), lambda i: (0, head)),
+            pl.BlockSpec((rows, block), lambda i: (0, first // count)),
             pl.BlockSpec((gathered.shape[0], 2 * head_size, gathered.shape[2]), lambda i: (0, head, 0)),
             pl.BlockSpec((gathered.shape[0], 16, gathered.shape[2]), lambda i: (0, id_row // 16, 0)),
             pl.BlockSpec(info.shape, lambda i: (0, 0)),
@@ -64,6 +65,13 @@
         out_specs=pl.BlockSpec((rows, block), lambda i: (0, 0)),
         out_shape=jax.ShapeDtypeStruct((rows, block), jnp.bfloat16),
     )(q, gathered, gathered, info)
+
+
+def chunk_plan(heads, kv_heads):
+    groups = heads // kv_heads
+    plan = [(0, groups // 2), (groups // 2, groups // 2)]
+    plan += [(h * groups, groups) for h in range(1, kv_heads)]
+    return plan
 
 
 def attend(queries, keys_values, segment_ids, bounds):
@@ -90,9 +98,9 @@
     info = jnp.stack([segments, query_pos, query_bound], axis=1).astype(jnp.int32)
 
     pieces = []
-    for h in range(kv_heads):
-        out_h = attention_head(query_rows, gathered, info, h, body_rows, kv_heads, head_size)
-        pieces.append(from_behind(out_h, "section", 1))
+    for first, count in chunk_plan(query_rows.shape[1] // head_size, kv_heads):
+        out_c = attention_head(query_rows, gathered, info, first, count, body_rows, kv_heads, head_size)
+        pieces.append(from_behind(out_c, "section", 1))
     return jnp.concatenate(pieces, axis=1)[None]
 
 

time: 217 us -> 201 us (0.926)
  the two profiles are of different devices: /device:TPU:1 before, /device:TPU:130 now
where the time goes in v7:
time: 201 us
  waiting for transfers between devices  122 us (61%)
  starting transfers between devices  38.5 us (19%)
  Pallas kernels  21.3 us (11%)
  between operations  13.5 us (7%)
  local copies, waits for them, and re-layouts  2.86 us (1%)
  other arithmetic  2.81 us (1%)
    all_gather x1, waiting for transfers between devices, attend(): gathered = lax.all_gather(packed, 'tensor', axis=0, tiled=False)  71.9 us
    ppermute x5, waiting for transfers between devices, from_behind(): return lax.ppermute(block, axis, route)  49.9 us
    ppermute x5, starting transfers between devices, from_behind(): return lax.ppermute(block, axis, route)  38.5 us
    pallas_call x5, Pallas kernels, attention_head(): pl.pallas_call(kernel, grid=(1,), in_specs=[pl.BlockSpec((rows, block), l...  21.3 us
  transfers between devices with their start and end apart: 6, of which 3 were waited for; matrix products, arithmetic and copies ran while one was open for 1% of the time, Pallas kernels for 9%

profile of v7, /device:TPU:130, one launch (start us, length us, event | category | flops | bytes accessed | tf_op | source)
XLA Modules:
  0.0 200.9 jit_solution(8258801276367670458)
XLA Ops:
  6.5 0.0 all-gather.3.cloned.1.call-start
  6.5 0.7 convert_element_type.4
  7.2 1.1 reshape_squeeze.3
  8.3 0.7 fusion.1
  9.0 0.0 all-gather.3.cloned.1.call-update
  9.1 0.8 select_reduce_fusion
  9.8 0.7 pad_add_fusion
  10.5 0.7 copy.15.i_ref
  11.2 71.9 %all-gather.3.cloned.1.call-done = bf16[8320,128]{1,0:T(8,128)(2,1)} async-done(((bf16[1040,128]{1,0:T(8,128)(2,1)}), bf16[8320,128]{1,0:T(8,128)(2,1)}) %all-gather.3.cloned.1.call-update) | async-done | bytes 2129936 | tf_op jit(solution)/shard_map/all_gather | solution.py:93
  83.1 3.4 %shard_map.46 = bf16[128,512]{1,0:T(8,128)(2,1)} custom-call(bf16[128,4096]{1,0:T(8,128)(2,1)} %bitcast.19, bf16[8,1040,128]{2,1,0:T(8,128)(2,1)} %bitcast.9, bf16[8,1040,128]{2,1,0:T(8,128)(2,1)} %bitcast.10, s32[128,3]{1,0:T(8,128)} %copy.15.i_ref), custom_call_target="tpu_custom_call" | custom-call | tf_op jit(solution)/shard_map/pallas_call | solution.py:56
  86.5 7.6 %collective-permute-start = (bf16[128,512]{1,0:T(8,128)(2,1)}, bf16[128,512]{1,0:T(8,128)(2,1)S(1)}, u32[]{:S(2)}, u32[]{:S(2)}) collective-permute-start(bf16[128,512]{1,0:T(8,128)(2,1)} %shard_map.46), channel_id=1, source_target_pairs={{960,0},{0,64},{64,128},{128,192},{192,256},{256,320},{320,384},{3... | collective-permute-start | bytes 393224 | tf_op jit(solution)/shard_map/ppermute | solution.py:14
  94.1 4.8 %shard_map.48 = bf16[128,1024]{1,0:T(8,128)(2,1)} custom-call(bf16[128,4096]{1,0:T(8,128)(2,1)} %bitcast.20, bf16[8,1040,128]{2,1,0:T(8,128)(2,1)} %bitcast.11, bf16[8,1040,128]{2,1,0:T(8,128)(2,1)} %bitcast.12, s32[128,3]{1,0:T(8,128)} %copy.15.i_ref), custom_call_target="tpu_custom_call" | custom-call | tf_op jit(solution)/shard_map/pallas_call | solution.py:56
  98.9 7.6 %collective-permute-start.2 = (bf16[128,1024]{1,0:T(8,128)(2,1)}, bf16[128,1024]{1,0:T(8,128)(2,1)S(1)}, u32[]{:S(2)}, u32[]{:S(2)}) collective-permute-start(bf16[128,1024]{1,0:T(8,128)(2,1)} %shard_map.48), channel_id=1, source_target_pairs={{960,0},{0,64},{64,128},{128,192},{192,256},{256,320},{320,384},{3... | collective-permute-start | bytes 786440 | tf_op jit(solution)/shard_map/ppermute | solution.py:14
  106.5 3.4 %shard_map.47 = bf16[128,512]{1,0:T(8,128)(2,1)} custom-call(bf16[128,4096]{1,0:T(8,128)(2,1)} %bitcast.21, bf16[8,1040,128]{2,1,0:T(8,128)(2,1)} %bitcast.13, bf16[8,1040,128]{2,1,0:T(8,128)(2,1)} %bitcast.14, s32[128,3]{1,0:T(8,128)} %copy.15.i_ref), custom_call_target="tpu_custom_call" | custom-call | tf_op jit(solution)/shard_map/pallas_call | solution.py:56
  109.9 8.3 %collective-permute-start.1 = (bf16[128,512]{1,0:T(8,128)(2,1)}, bf16[128,512]{1,0:T(8,128)(2,1)S(1)}, u32[]{:S(2)}, u32[]{:S(2)}) collective-permute-start(bf16[128,512]{1,0:T(8,128)(2,1)} %shard_map.47), channel_id=1, source_target_pairs={{960,0},{0,64},{64,128},{128,192},{192,256},{256,320},{320,384},{3... | collective-permute-start | bytes 393224 | tf_op jit(solution)/shard_map/ppermute | solution.py:14
  118.2 4.8 %shard_map.50 = bf16[128,1024]{1,0:T(8,128)(2,1)} custom-call(bf16[128,4096]{1,0:T(8,128)(2,1)} %bitcast.22, bf16[8,1040,128]{2,1,0:T(8,128)(2,1)} %bitcast.15, bf16[8,1040,128]{2,1,0:T(8,128)(2,1)} %bitcast.16, s32[128,3]{1,0:T(8,128)} %copy.15.i_ref), custom_call_target="tpu_custom_call" | custom-call | tf_op jit(solution)/shard_map/pallas_call | solution.py:56
  123.0 0.0 copy-start
  123.0 4.9 %shard_map.49 = bf16[128,1024]{1,0:T(8,128)(2,1)} custom-call(bf16[128,4096]{1,0:T(8,128)(2,1)} %bitcast.23, bf16[8,1040,128]{2,1,0:T(8,128)(2,1)} %bitcast.17, bf16[8,1040,128]{2,1,0:T(8,128)(2,1)} %bitcast.18, s32[128,3]{1,0:T(8,128)} %copy.15.i_ref), custom_call_target="tpu_custom_call" | custom-call | tf_op jit(solution)/shard_map/pallas_call | solution.py:56
  127.9 7.8 %collective-permute-start.3 = (bf16[128,1024]{1,0:T(8,128)(2,1)}, bf16[128,1024]{1,0:T(8,128)(2,1)S(1)}, u32[]{:S(2)}, u32[]{:S(2)}) collective-permute-start(bf16[128,1024]{1,0:T(8,128)(2,1)} %shard_map.49), channel_id=1, source_target_pairs={{960,0},{0,64},{64,128},{128,192},{192,256},{256,320},{320,384},{3... | collective-permute-start | bytes 786440 | tf_op jit(solution)/shard_map/ppermute | solution.py:14
  135.7 0.0 copy-done
  135.8 7.3 %collective-permute-start.4 = (bf16[128,1024]{1,0:T(8,128)(2,1)S(1)}, bf16[128,1024]{1,0:T(8,128)(2,1)S(1)}, u32[]{:S(2)}, u32[]{:S(2)}) collective-permute-start(bf16[128,1024]{1,0:T(8,128)(2,1)S(1)} %copy-done), channel_id=1, source_target_pairs={{960,0},{0,64},{64,128},{128,192},{192,256},{256,320},{320,384},{3... | collective-permute-start | bytes 786440 | tf_op jit(solution)/shard_map/ppermute | solution.py:14
  143.0 0.0 collective-permute-done
  143.0 0.0 collective-permute-done.1
  143.1 0.0 collective-permute-done.2
  143.1 44.5 %collective-permute-done.3 = bf16[128,1024]{1,0:T(8,128)(2,1)S(1)} collective-permute-done((bf16[128,1024]{1,0:T(8,128)(2,1)}, bf16[128,1024]{1,0:T(8,128)(2,1)S(1)}, u32[]{:S(2)}, u32[]{:S(2)}) %collective-permute-start.3) | collective-permute-done | bytes 262176 | tf_op jit(solution)/shard_map/ppermute | solution.py:14
  187.6 5.4 %collective-permute-done.4 = bf16[128,1024]{1,0:T(8,128)(2,1)S(1)} collective-permute-done((bf16[128,1024]{1,0:T(8,128)(2,1)S(1)}, bf16[128,1024]{1,0:T(8,128)(2,1)S(1)}, u32[]{:S(2)}, u32[]{:S(2)}) %collective-permute-start.4) | collective-permute-done | bytes 262176 | tf_op jit(solution)/shard_map/ppermute | solution.py:14
  193.0 0.0 copy-start.1
  193.1 1.0 copy-done.1
  (7 shorter events, 0.1 us)
Async XLA Ops:
  6.5 76.6 %all-gather.3.cloned.1.call-start = ((), (), s32[]{:S(2)}) async-start(), calls=%async_computation | async-start | bytes 2396160 | tf_op jit(solution)/shard_map/all_gather | solution.py:93
  86.5 56.5 %collective-permute-start = (bf16[128,512]{1,0:T(8,128)(2,1)}, bf16[128,512]{1,0:T(8,128)(2,1)S(1)}, u32[]{:S(2)}, u32[]{:S(2)}) collective-permute-start(bf16[128,512]{1,0:T(8,128)(2,1)} %shard_map.46), channel_id=1, source_target_pairs={{960,0},{0,64},{64,128},{128,192},{192,256},{256,320},{320,384},{3... | collective-permute-start | bytes 393224 | tf_op jit(solution)/shard_map/ppermute | solution.py:14
  98.9 44.1 %collective-permute-start.2 = (bf16[128,1024]{1,0:T(8,128)(2,1)}, bf16[128,1024]{1,0:T(8,128)(2,1)S(1)}, u32[]{:S(2)}, u32[]{:S(2)}) collective-permute-start(bf16[128,1024]{1,0:T(8,128)(2,1)} %shard_map.48), channel_id=1, source_target_pairs={{960,0},{0,64},{64,128},{128,192},{192,256},{256,320},{320,384},{3... | collective-permute-start | bytes 786440 | tf_op jit(solution)/shard_map/ppermute | solution.py:14
  109.9 33.1 %collective-permute-start.1 = (bf16[128,512]{1,0:T(8,128)(2,1)}, bf16[128,512]{1,0:T(8,128)(2,1)S(1)}, u32[]{:S(2)}, u32[]{:S(2)}) collective-permute-start(bf16[128,512]{1,0:T(8,128)(2,1)} %shard_map.47), channel_id=1, source_target_pairs={{960,0},{0,64},{64,128},{128,192},{192,256},{256,320},{320,384},{3... | collective-permute-start | bytes 393224 | tf_op jit(solution)/shard_map/ppermute | solution.py:14
  123.0 12.7 %copy-start = (bf16[128,1024]{1,0:T(8,128)(2,1)S(1)}, bf16[128,1024]{1,0:T(8,128)(2,1)}, u32[]{:S(2)}) copy-start(bf16[128,1024]{1,0:T(8,128)(2,1)} %shard_map.50) | copy-start | bytes 786436
  127.9 59.7 %collective-permute-start.3 = (bf16[128,1024]{1,0:T(8,128)(2,1)}, bf16[128,1024]{1,0:T(8,128)(2,1)S(1)}, u32[]{:S(2)}, u32[]{:S(2)}) collective-permute-start(bf16[128,1024]{1,0:T(8,128)(2,1)} %shard_map.49), channel_id=1, source_target_pairs={{960,0},{0,64},{64,128},{128,192},{192,256},{256,320},{320,384},{3... | collective-permute-start | bytes 786440 | tf_op jit(solution)/shard_map/ppermute | solution.py:14
  135.8 57.3 %collective-permute-start.4 = (bf16[128,1024]{1,0:T(8,128)(2,1)S(1)}, bf16[128,1024]{1,0:T(8,128)(2,1)S(1)}, u32[]{:S(2)}, u32[]{:S(2)}) collective-permute-start(bf16[128,1024]{1,0:T(8,128)(2,1)S(1)} %copy-done), channel_id=1, source_target_pairs={{960,0},{0,64},{64,128},{128,192},{192,256},{256,320},{320,384},{3... | collective-permute-start | bytes 786440 | tf_op jit(solution)/shard_map/ppermute | solution.py:14
  193.0 1.0 copy-start.1
Sparse Core Ops, SparseCore 0:
  10.0 73.0 all-gather.2
